TPU v7x, 128 devices: a whole 4x4x4 slice. The times are simulated.
128 devices in a mesh: row: 16 (over y, x_hi, core), col: 8 (over x_lo, z).
Axes of the slice: x: 4 (x_hi: 2, x_lo: 2; x = x_hi * 2 + x_lo), y: 4, z: 4, core: 2. Of those that a mesh axis runs over, the one named last changes fastest.
Arguments:
- matrix: float32 [24576, 4, 3072], P('row', None, 'col'), may hold values from -60 to 60, as said below
Outputs:
- factored: float32 [24576, 4, 3072], P('row', None, 'col')
- r_rows: float32 [2, 384, 4, 3072], P(None, None, None, 'col')
Inputs may be any that keep to these rules, and one draw needn't show every extreme that they name: `matrix`: dense real entries with column scales that differ from column to column.
All inputs are finite; a program needn't handle non-finite values.
Results may differ from a plain program's by a relative error of at most 0.00017.
Values sent between devices are 32-bit elements; how exact they have to be, the bound alone decides.
No kernel may reach another device: no remote copies, remote signals or barrier semaphores. Data moves between devices by JAX's collectives and lax.ppermute only.
A program may use at most 128 MiB of HBM per device.

v0:
```python
import jax
import jax.numpy as jnp
from jax import lax
from jax.sharding import PartitionSpec as P

STEPS = 2


def spread(block, axis, holder):
    block = jnp.where(lax.axis_index(axis) == holder, block, jnp.zeros_like(block))
    return lax.psum(block, axis)


def shards(matrix):
    highest = lax.Precision.HIGHEST
    ncol = lax.axis_size("col")
    column = lax.axis_index("col")
    count = matrix.shape[1]
    width = matrix.shape[2]
    glob = jnp.arange(count, dtype=jnp.int32) * ncol + column
    ident = jnp.eye(width, dtype=jnp.float32)
    blocks = matrix
    rows_out = []
    for k in range(STEPS):
        owner = k % ncol
        local_index = k // ncol
        local_panel = blocks[:, local_index, :]
        gram = lax.psum(
            jnp.dot(
                local_panel.T, local_panel, precision=highest, preferred_element_type=jnp.float32
            ),
            "row",
        )
        lower = jnp.linalg.cholesky(gram)
        inverse = lax.linalg.triangular_solve(lower, ident, left_side=True, lower=True)
        own_basis = jnp.dot(
            local_panel, inverse.T, precision=highest, preferred_element_type=jnp.float32
        )
        basis = spread(own_basis, "col", owner)
        partial_proj = jnp.einsum("mb,mjt->bjt", basis, blocks, precision=highest)
        proj = lax.psum(partial_proj, "row")
        kept = jnp.where((glob > k)[None, :, None], proj, jnp.float32(0.0))
        blocks = blocks - jnp.einsum("mb,bjt->mjt", basis, kept, precision=highest)
        is_panel = (glob == k)[None, :, None]
        blocks = jnp.where(is_panel, basis[:, None, :], blocks)
        rows_out.append(jnp.where(is_panel, lower.T[:, None, :], kept))
    return (blocks, jnp.stack(rows_out))


def solution(mesh):
    return jax.shard_map(
        shards,
        mesh=mesh,
        in_specs=(P("row", None, "col"),),
        out_specs=(P("row", None, "col"), P(None, None, None, "col")),
        check_vma=False,
    )
```

profile of v0, /device:TPU:0, one launch (start us, length us, event | category | flops | bytes accessed | tf_op | source)
XLA Modules:
  0.0 1087.4 jit_solution(16035788120656499901)
XLA Ops:
  7.2 4.3 copy.16
  15.2 4.8 fusion.7
  20.7 141.6 %all-reduce.8.cloned.1.call-done = f32[384,384]{0,1:T(8,128)} async-done(((f32[384,384]{0,1:T(8,128)}), f32[384,384]{0,1:T(8,128)}) %all-reduce.8.cloned.1.call-update) | async-done | bytes 589840 | tf_op jit(solution)/shard_map/psum | solution.py:28
  164.7 11.7 %cholesky.208 = f32[128,128]{1,0:T(8,128)S(1)} custom-call(f32[128,128]{1,0:T(8,128)S(1)} %cholesky.310), custom_call_target="Cholesky" | custom-call | tf_op jit(solution)/shard_map/jit(cholesky)/cholesky | solution.py:34
  176.4 9.8 custom-call.20
  186.9 11.7 %cholesky.227 = f32[128,128]{1,0:T(8,128)S(1)} custom-call(f32[128,128]{1,0:T(8,128)S(1)} %cholesky.314), custom_call_target="Cholesky" | custom-call | tf_op jit(solution)/shard_map/jit(cholesky)/cholesky | solution.py:34
  198.6 10.0 custom-call.21
  209.1 11.7 %cholesky.246 = f32[128,128]{1,0:T(8,128)S(1)} custom-call(f32[128,128]{1,0:T(8,128)S(1)} %convolution_subtract_fusion.7), custom_call_target="Cholesky" | custom-call | tf_op jit(solution)/shard_map/jit(cholesky)/cholesky | solution.py:34
  224.2 6.4 while.4
  230.6 29.5 %custom-call.22 = f32[3,128,128]{1,2,0:T(8,128)S(1)} custom-call(f32[3,128,128]{2,1,0:T(8,128)S(1)} %get-tuple-element.18), custom_call_target="InvertDiagBlocksLowerTriangular" | custom-call | tf_op jit(solution)/shard_map/triangular_solve/custom-call.2 | solution.py:35
  261.9 7.0 fusion
  269.0 81.4 %all-reduce.10.cloned.1.call-done = f32[1536,384]{0,1:T(8,128)} async-done(((f32[1536,384]{0,1:T(8,128)}), f32[1536,384]{0,1:T(8,128)}) %all-reduce.10.cloned.1.call-update) | async-done | bytes 2359312 | tf_op jit(solution)/shard_map/psum | solution.py:11
  350.4 16.7 %fusion.4 = f32[384,4,384]{2,0,1:T(8,128)} fusion(f32[1536,384]{0,1:T(8,128)} %all-reduce.10.cloned.1.call-done, f32[1536,4,384]{2,1,0:T(4,128)} %param.4), kind=kOutput, calls=%fused_computation.15 | convolution fusion | flops 10871635968 | bytes 14155776 | tf_op jit(solution)/shard_map/mb,mjt->bjt/dot_general | solution.py:40
  369.3 145.5 %all-reduce.12.cloned.1.call-done = f32[384,4,384]{2,0,1:T(8,128)} async-done(((f32[384,4,384]{2,0,1:T(8,128)}), f32[384,4,384]{2,0,1:T(8,128)}) %all-reduce.12.cloned.1.call-update) | async-done | bytes 2359312 | tf_op jit(solution)/shard_map/psum | solution.py:41
  514.8 21.5 %subtract_select_fusion.1 = f32[1536,4,384]{2,0,1:T(8,128)S(1)} fusion(f32[1536,384]{1,0:T(8,128)S(1)} %copy.19, pred[4]{0:T(512)(128)(4,1)S(1)} %get-tuple-element.67, f32[1536,384]{0,1:T(8,128)} %all-reduce.10.cloned.1.call-done, f32[384,4,384]{2,0,1:T(8,128)} %all-reduce.12.cloned.1.call-done, pred[4]{0:T(512)(128)(4,1)S(1)} %get-tuple-element.66, ...), kind=kOutput, calls=%fused_computation.5 | convolution fusion | flops 10876944384 | bytes 25952264 | tf_op jit(solution)/shard_map/mb,bjt->mjt/dot_general | solution.py:43
  536.4 3.7 copy-done
  540.1 4.8 fusion.8
  545.0 139.8 %all-reduce.14.cloned.1.call-done = f32[384,384]{0,1:T(8,128)} async-done(((f32[384,384]{0,1:T(8,128)}), f32[384,384]{0,1:T(8,128)}) %all-reduce.14.cloned.1.call-update) | async-done | bytes 589840 | tf_op jit(solution)/shard_map/psum | solution.py:28
  687.3 11.7 %cholesky.261 = f32[128,128]{1,0:T(8,128)S(1)} custom-call(f32[128,128]{1,0:T(8,128)S(1)} %cholesky.318), custom_call_target="Cholesky" | custom-call | tf_op jit(solution)/shard_map/jit(cholesky)/cholesky | solution.py:34
  699.7 9.8 custom-call.23
  710.1 11.7 %cholesky.280 = f32[128,128]{1,0:T(8,128)S(1)} custom-call(f32[128,128]{1,0:T(8,128)S(1)} %cholesky.322), custom_call_target="Cholesky" | custom-call | tf_op jit(solution)/shard_map/jit(cholesky)/cholesky | solution.py:34
  722.5 10.2 custom-call.24
  733.2 11.7 %cholesky.299 = f32[128,128]{1,0:T(8,128)S(1)} custom-call(f32[128,128]{1,0:T(8,128)S(1)} %convolution_subtract_fusion.6), custom_call_target="Cholesky" | custom-call | tf_op jit(solution)/shard_map/jit(cholesky)/cholesky | solution.py:34
  748.3 6.1 while.5
  754.5 29.5 %custom-call.25 = f32[3,128,128]{1,2,0:T(8,128)S(1)} custom-call(f32[3,128,128]{2,1,0:T(8,128)S(1)} %get-tuple-element.19), custom_call_target="InvertDiagBlocksLowerTriangular" | custom-call | tf_op jit(solution)/shard_map/triangular_solve/custom-call.2 | solution.py:35
  785.8 6.9 convolution_select_fusion
  792.8 81.4 %all-reduce.16.cloned.1.call-done = f32[1536,384]{1,0:T(8,128)} async-done(((f32[1536,384]{1,0:T(8,128)}), f32[1536,384]{1,0:T(8,128)}) %all-reduce.16.cloned.1.call-update) | async-done | bytes 2359312 | tf_op jit(solution)/shard_map/psum | solution.py:11
  874.2 16.2 %fusion.1 = f32[384,4,384]{2,0,1:T(8,128)} fusion(f32[1536,4,384]{2,0,1:T(8,128)} %copy-done, f32[1536,384]{1,0:T(8,128)} %all-reduce.16.cloned.1.call-done), kind=kOutput, calls=%fused_computation.12 | convolution fusion | flops 10871635968 | bytes 14155776 | tf_op jit(solution)/shard_map/mb,mjt->bjt/dot_general | solution.py:40
  895.3 142.8 %all-reduce.18.cloned.1.call-done = f32[384,4,384]{2,0,1:T(8,128)} async-done(((f32[384,4,384]{2,0,1:T(8,128)}), f32[384,4,384]{2,0,1:T(8,128)}) %all-reduce.18.cloned.1.call-update) | async-done | bytes 2359312 | tf_op jit(solution)/shard_map/psum | solution.py:41
  1040.8 5.4 copy.29
  1047.4 16.5 %subtract_select_fusion = f32[1536,4,384]{2,0,1:T(8,128)S(1)} fusion(f32[1536,4,384]{2,0,1:T(8,128)S(1)} %bitcast.110, f32[1536,384]{1,0:T(8,128)S(1)} %copy-done.2, pred[4]{0:T(512)(128)(4,1)S(1)} %get-tuple-element.69, f32[384,4,384]{2,0,1:T(8,128)S(1)} %copy-done.4, pred[4]{0:T(512)(128)(4,1)S(1)} %get-tuple-element.68), kind=kOutput, calls=%fused_computation.4 | convolution fusion | flops 10876944384 | bytes 23592968 | tf_op jit(solution)/shard_map/mb,bjt->mjt/dot_general | solution.py:43
  1063.9 16.5 %copy.28 = f32[1536,4,384]{2,1,0:T(4,128)} copy(f32[1536,4,384]{2,0,1:T(8,128)S(1)} %subtract_select_fusion) | data formatting | bytes 18874368
  (104 shorter events, 42.8 us)
Async XLA Ops:
  7.2 155.1 %all-reduce.8.cloned.1.call-start = ((), (), s32[]{:S(2)}) async-start(), calls=%async_computation | async-start | bytes 1179648 | tf_op jit(solution)/shard_map/psum | solution.py:28
  11.5 3.7 copy-start.1
  20.1 330.3 %all-reduce.10.cloned.1.call-start = ((), (), s32[]{:S(2)}) async-start(), calls=%async_computation.1 | async-start | bytes 4718592 | tf_op jit(solution)/shard_map/psum | solution.py:11
  268.9 245.9 %all-reduce.12.cloned.1.call-start = ((), (), s32[]{:S(2)}) async-start(), calls=%async_computation.2 | async-start | bytes 4718592 | tf_op jit(solution)/shard_map/psum | solution.py:41
  367.2 317.7 %all-reduce.14.cloned.1.call-start = ((), (), s32[]{:S(2)}) async-start(), calls=%async_computation.3 | async-start | bytes 1179648 | tf_op jit(solution)/shard_map/psum | solution.py:28
  536.4 3.7 copy-start
  545.0 329.2 %all-reduce.16.cloned.1.call-start = ((), (), s32[]{:S(2)}) async-start(), calls=%async_computation.4 | async-start | bytes 4718592 | tf_op jit(solution)/shard_map/psum | solution.py:11
  792.8 245.4 %all-reduce.18.cloned.1.call-start = ((), (), s32[]{:S(2)}) async-start(), calls=%async_computation.5 | async-start | bytes 4718592 | tf_op jit(solution)/shard_map/psum | solution.py:41
  890.4 1.9 copy-start.3
  892.3 2.8 copy-start.6
  1038.1 2.4 copy-start.5
  1040.5 5.8 slice-start
  1040.5 5.8 slice-start.1
  1040.8 5.5 slice-start.2
  1040.8 5.5 copy-start.2
  1040.8 6.6 copy-start.4
Sparse Core Ops, SparseCore 0:
  20.2 141.9 all-reduce.7
  269.1 81.3 all-reduce.9
  367.3 147.4 all-reduce.11
  545.1 139.7 all-reduce.13
  792.9 81.2 all-reduce.15
  890.6 147.5 all-reduce.17
where the time goes:
time: 1090 us
  waiting for transfers between devices  733 us (67%)
  other arithmetic  181 us (17%)
  matrix products  100 us (9%)
  local copies, waits for them, and re-layouts  54.3 us (5%)
  between operations  18.5 us (2%)
    psum x2, waiting for transfers between devices, shards(): proj = lax.psum(partial_proj, 'row')  288 us
    psum x2, waiting for transfers between devices, shards(): lax.psum(jnp.dot(local_panel.T, local_panel, precision=highest, preferred...  281 us
    psum x2, waiting for transfers between devices, spread(): return lax.psum(block, axis)  163 us
    another operation x21, other arithmetic, shards(): lower = jnp.linalg.cholesky(gram)  114 us
    another operation x3, other arithmetic, shards(): lax.linalg.triangular_solve(lower, ident, left_side=True, lower=True)  59 us
    dot_general x2, matrix products, shards(): blocks = blocks - jnp.einsum('mb,bjt->mjt', basis, kept, precision=highest)  38 us
    unnamed x23, local copies, waits for them, and re-layouts  35.9 us
    dot_general x2, matrix products, shards(): partial_proj = jnp.einsum('mb,mjt->bjt', basis, blocks, precision=highest)  32.9 us
  transfers between devices with their start and end apart: 6, of which 6 were waited for; matrix products, arithmetic and copies ran while one was open for 1% of the time, Pallas kernels for 0%

commit v1 on v0

v1 whole, which is shorter than its diff:
```python
import jax
import jax.numpy as jnp
from jax import lax
from jax.sharding import PartitionSpec as P

STEPS = 2


def shards(matrix):
    highest = lax.Precision.HIGHEST
    column = lax.axis_index("col")
    ncol = lax.axis_size("col")
    count = matrix.shape[1]
    width = matrix.shape[2]
    glob = jnp.arange(count, dtype=jnp.int32) * ncol + column
    ident = jnp.eye(width, dtype=jnp.float32)
    own = matrix[:, 0, :]
    zero = jnp.zeros_like(own)
    both = lax.psum(
        jnp.concatenate(
            [jnp.where(column == 0, own, zero), jnp.where(column == 1, own, zero)], axis=1
        ),
        "col",
    )
    gram_part = jnp.dot(both.T, both, precision=highest, preferred_element_type=jnp.float32)
    cross_part = jnp.einsum("mb,mjt->bjt", both, matrix, precision=highest)
    gram, cross = lax.psum((gram_part, cross_part), "row")
    g00 = gram[:width, :width]
    g10 = gram[width:, :width]
    g11 = gram[width:, width:]
    lower0 = jnp.linalg.cholesky(g00)
    inv0 = lax.linalg.triangular_solve(lower0, ident, left_side=True, lower=True)
    xmat = jnp.dot(g10, inv0.T, precision=highest, preferred_element_type=jnp.float32)
    schur = g11 - jnp.dot(xmat, xmat.T, precision=highest, preferred_element_type=jnp.float32)
    lower1 = jnp.linalg.cholesky(schur)
    inv1 = lax.linalg.triangular_solve(lower1, ident, left_side=True, lower=True)
    proj0 = jnp.einsum("ab,bjt->ajt", inv0, cross[:width], precision=highest)
    rest1 = cross[width:] - jnp.einsum("ab,bjt->ajt", xmat, proj0, precision=highest)
    proj1 = jnp.einsum("ab,bjt->ajt", inv1, rest1, precision=highest)
    panel0 = both[:, :width]
    panel1 = both[:, width:]
    basis0 = jnp.dot(panel0, inv0.T, precision=highest, preferred_element_type=jnp.float32)
    resid1 = panel1 - jnp.dot(basis0, xmat.T, precision=highest, preferred_element_type=jnp.float32)
    basis1 = jnp.dot(resid1, inv1.T, precision=highest, preferred_element_type=jnp.float32)
    kept0 = jnp.where((glob > 0)[None, :, None], proj0, jnp.float32(0.0))
    kept1 = jnp.where((glob > 1)[None, :, None], proj1, jnp.float32(0.0))
    basis = jnp.concatenate([basis0, basis1], axis=1)
    kept = jnp.concatenate([kept0, kept1], axis=0)
    blocks = matrix - jnp.einsum("mb,bjt->mjt", basis, kept, precision=highest)
    blocks = jnp.where((glob == 0)[None, :, None], basis0[:, None, :], blocks)
    blocks = jnp.where((glob == 1)[None, :, None], basis1[:, None, :], blocks)
    row0 = jnp.where((glob == 0)[None, :, None], lower0.T[:, None, :], kept0)
    row1 = jnp.where((glob == 1)[None, :, None], lower1.T[:, None, :], kept1)
    return (blocks, jnp.stack([row0, row1]))


def solution(mesh):
    return jax.shard_map(
        shards,
        mesh=mesh,
        in_specs=(P("row", None, "col"),),
        out_specs=(P("row", None, "col"), P(None, None, None, "col")),
        check_vma=False,
    )
```

time: 1090 us -> 673 us (0.62)
  waiting for transfers between devices: 733 us -> 292 us
  matrix products: 100 us -> 116 us
    psum x6 -> x2, waiting for transfers between devices: 733 us -> 292 us  [the longest x1 174 us: shards(): gram, cross = lax.psum((gram_part, cross_part), 'row')]
    dot_general x8 -> x11, matrix products: 94.5 us -> 110 us  [the longest x1 27.3 us: shards(): blocks = matrix - jnp.einsum('mb,bjt->mjt', basis, kept, precision=highest)]
    unnamed x23 -> x29, local copies, waits for them, and re-layouts: 35.9 us -> 31.2 us
  transfers between devices with their start and end apart: 6 -> 2, of which waited for: 6 -> 2; matrix products, arithmetic and copies ran while one was open for 1% -> 0% of each run, Pallas kernels for 0% -> 0%
where the time goes in v1:
time: 673 us; the launch traced here: 665 us
  waiting for transfers between devices  292 us (43%)
  other arithmetic  184 us (27%)
  matrix products  116 us (17%)
  local copies, waits for them, and re-layouts  53.4 us (8%)
  between operations  18.9 us (3%)
    psum x1, waiting for transfers between devices, shards(): gram, cross = lax.psum((gram_part, cross_part), 'row')  174 us
    psum x1, waiting for transfers between devices, shards(): lax.psum(jnp.concatenate([jnp.where(column == 0, own, zero), jnp.where(co...  118 us
    another operation x11, other arithmetic, shards(): lower1 = jnp.linalg.cholesky(schur)  57.1 us
    another operation x10, other arithmetic, shards(): lower0 = jnp.linalg.cholesky(g00)  56.6 us
    unnamed x29, local copies, waits for them, and re-layouts  31.2 us
    another operation x1, other arithmetic, shards(): lax.linalg.triangular_solve(lower1, ident, left_side=True, lower=True)  29.9 us
    another operation x2, other arithmetic, shards(): lax.linalg.triangular_solve(lower0, ident, left_side=True, lower=True)  29.7 us
    dot_general x1, matrix products, shards(): blocks = matrix - jnp.einsum('mb,bjt->mjt', basis, kept, precision=highest)  27.3 us
  transfers between devices with their start and end apart: 2, of which 2 were waited for; matrix products, arithmetic and copies ran while one was open for 0% of the time, Pallas kernels for 0%

profile of v1, /device:TPU:0, one launch (start us, length us, event | category | flops | bytes accessed | tf_op | source)
XLA Modules:
  0.0 664.7 jit_solution(6891824529621162011)
XLA Ops:
  8.9 5.1 copy.21
  16.2 2.5 pad_maximum_fusion
  18.8 118.0 %all-reduce.5.cloned.1.call-done = f32[1536,768]{0,1:T(8,128)} async-done(((f32[1536,768]{0,1:T(8,128)}), f32[1536,768]{0,1:T(8,128)}) %all-reduce.5.cloned.1.call-update) | async-done | bytes 4718608 | tf_op jit(solution)/shard_map/psum | solution.py:19
  136.8 15.8 %fusion.71 = f32[768,768]{0,1:T(8,128)} fusion(f32[1536,768]{0,1:T(8,128)} %all-reduce.5.cloned.1.call-done), kind=kOutput, calls=%fused_computation.140 | convolution fusion | flops 10871635968 | bytes 7077888 | tf_op jit(solution)/shard_map/dot_general | solution.py:25
  152.6 26.1 %fusion = f32[768,4,384]{2,0,1:T(8,128)} fusion(f32[1536,4,384]{2,1,0:T(4,128)} %param.4, f32[1536,768]{0,1:T(8,128)S(1)} %copy-done.8), kind=kOutput, calls=%fused_computation.5 | convolution fusion | flops 21743271936 | bytes 18874368 | tf_op jit(solution)/shard_map/mb,mjt->bjt/dot_general | solution.py:26
  179.2 174.2 %all-reduce.7.cloned.1.call-done = (f32[768,768]{0,1:T(8,128)}, f32[768,4,384]{2,0,1:T(8,128)}) async-done(((f32[768,768]{0,1:T(8,128)}, f32[768,4,384]{2,0,1:T(8,128)}), (f32[768,768]{0,1:T(8,128)}, f32[768,4,384]{2,0,1:T(8,128)})) %all-reduce.7.cloned.1.call-update) | async-done | bytes 7077904 | tf_op jit(solution)/shard_map/psum | solution.py:27
  355.9 11.7 %cholesky.208 = f32[128,128]{1,0:T(8,128)S(1)} custom-call(f32[128,128]{1,0:T(8,128)S(1)} %cholesky.310), custom_call_target="Cholesky" | custom-call | tf_op jit(solution)/shard_map/jit(cholesky)/cholesky | solution.py:31
  367.7 9.8 %custom-call.20 = f32[1,128,128]{1,2,0:T(8,128)S(1)} custom-call(f32[1,128,128]{2,1,0:T(8,128)S(1)} %get-tuple-element.65), custom_call_target="InvertDiagBlocksLowerTriangular" | custom-call | tf_op jit(solution)/shard_map/jit(cholesky)/cholesky | solution.py:31
  378.1 11.7 %cholesky.227 = f32[128,128]{1,0:T(8,128)S(1)} custom-call(f32[128,128]{1,0:T(8,128)S(1)} %cholesky.314), custom_call_target="Cholesky" | custom-call | tf_op jit(solution)/shard_map/jit(cholesky)/cholesky | solution.py:31
  389.9 10.2 %custom-call.21 = f32[1,128,128]{1,2,0:T(8,128)S(1)} custom-call(f32[1,128,128]{2,1,0:T(8,128)S(1)} %get-tuple-element.62), custom_call_target="InvertDiagBlocksLowerTriangular" | custom-call | tf_op jit(solution)/shard_map/jit(cholesky)/cholesky | solution.py:31
  400.6 11.7 %cholesky.246 = f32[128,128]{1,0:T(8,128)S(1)} custom-call(f32[128,128]{1,0:T(8,128)S(1)} %convolution_subtract_fusion.9), custom_call_target="Cholesky" | custom-call | tf_op jit(solution)/shard_map/jit(cholesky)/cholesky | solution.py:31
  416.5 6.3 while.4
  422.8 29.7 %custom-call.22 = f32[3,128,128]{1,2,0:T(8,128)S(1)} custom-call(f32[3,128,128]{2,1,0:T(8,128)S(1)} %get-tuple-element.18), custom_call_target="InvertDiagBlocksLowerTriangular" | custom-call | tf_op jit(solution)/shard_map/triangular_solve/custom-call.2 | solution.py:32
  454.4 3.1 fusion.14
  457.5 2.3 convolution_subtract_fusion.1
  460.1 11.7 %cholesky.261 = f32[128,128]{1,0:T(8,128)S(1)} custom-call(f32[128,128]{1,0:T(8,128)S(1)} %cholesky.318), custom_call_target="Cholesky" | custom-call | tf_op jit(solution)/shard_map/jit(cholesky)/cholesky | solution.py:35
  471.9 9.8 %custom-call.23 = f32[1,128,128]{1,2,0:T(8,128)S(1)} custom-call(f32[1,128,128]{2,1,0:T(8,128)S(1)} %get-tuple-element.58), custom_call_target="InvertDiagBlocksLowerTriangular" | custom-call | tf_op jit(solution)/shard_map/jit(cholesky)/cholesky | solution.py:35
  482.3 11.9 %cholesky.280 = f32[128,128]{1,0:T(8,128)S(1)} custom-call(f32[128,128]{1,0:T(8,128)S(1)} %cholesky.322), custom_call_target="Cholesky" | custom-call | tf_op jit(solution)/shard_map/jit(cholesky)/cholesky | solution.py:35
  494.2 9.8 %custom-call.24 = f32[1,128,128]{1,2,0:T(8,128)S(1)} custom-call(f32[1,128,128]{2,1,0:T(8,128)S(1)} %get-tuple-element.55), custom_call_target="InvertDiagBlocksLowerTriangular" | custom-call | tf_op jit(solution)/shard_map/jit(cholesky)/cholesky | solution.py:35
  504.6 11.7 %cholesky.299 = f32[128,128]{1,0:T(8,128)S(1)} custom-call(f32[128,128]{1,0:T(8,128)S(1)} %convolution_subtract_fusion.8), custom_call_target="Cholesky" | custom-call | tf_op jit(solution)/shard_map/jit(cholesky)/cholesky | solution.py:35
  521.2 6.1 while.5
  527.3 29.9 %custom-call.25 = f32[3,128,128]{1,2,0:T(8,128)S(1)} custom-call(f32[3,128,128]{2,1,0:T(8,128)S(1)} %get-tuple-element.19), custom_call_target="InvertDiagBlocksLowerTriangular" | custom-call | tf_op jit(solution)/shard_map/triangular_solve/custom-call.2 | solution.py:36
  559.0 5.6 fusion.9
  564.7 5.4 fusion.16
  571.2 7.0 %fusion.11 = f32[1536,384]{0,1:T(8,128)} fusion(f32[1536,768]{0,1:T(8,128)} %all-reduce.5.cloned.1.call-done, f32[128,384]{1,0:T(8,128)S(1)} %fusion.52, f32[128,384]{1,0:T(8,128)S(1)} %fusion.54, f32[128,384]{1,0:T(8,128)S(1)} %fusion.37), kind=kOutput, calls=%fused_computation.21 | convolution fusion | flops 2718203904 | bytes 5308416 | tf_op jit(solution)/shard_map/dot_general | solution.py:42
  580.3 6.4 convolution_subtract_fusion
  586.8 5.4 fusion.28
  592.1 3.1 copy.8
  595.2 6.1 fusion.13
  606.2 27.3 %select_select_fusion = f32[1536,4,384]{2,0,1:T(8,128)S(1)} fusion(f32[1536,4,384]{2,1,0:T(4,128)} %param.4, f32[1536,384]{0,1:T(8,128)S(1)} %copy-done.2, f32[1536,384]{0,1:T(8,128)S(1)} %copy-done.1, f32[384,4,384]{2,0,1:T(8,128)S(1)} %fusion.13, f32[384,4,384]{2,0,1:T(8,128)S(1)} %get-tuple-element.41, f32[1536,384]{1,0:T(8,128)S(1)} %copy.9, ...), kind=kOutput, calls=%fused_computation.4 | convolution fusion | flops 21752709120 | bytes 33030152 | tf_op jit(solution)/shard_map/mb,bjt->mjt/dot_general | solution.py:49
  633.5 16.5 %copy.15 = f32[1536,4,384]{2,1,0:T(4,128)} copy(f32[1536,4,384]{2,0,1:T(8,128)S(1)} %select_select_fusion) | data formatting | bytes 18874368
  652.2 5.2 copy.16
  (107 shorter events, 41.0 us)
Async XLA Ops:
  7.2 129.6 %all-reduce.5.cloned.1.call-start = ((), (), s32[]{:S(2)}) async-start(), calls=%async_computation | async-start | bytes 9437184 | tf_op jit(solution)/shard_map/psum | solution.py:19
  7.2 1.7 slice-start
  18.8 334.7 %all-reduce.7.cloned.1.call-start = ((), (), s32[]{:S(2)}) async-start(), calls=%async_computation.1 | async-start | bytes 14155776 | tf_op jit(solution)/shard_map/psum | solution.py:27
  136.8 15.8 %copy-start.8 = (f32[1536,768]{0,1:T(8,128)S(1)}, f32[1536,768]{0,1:T(8,128)}, u32[]{:S(2)}) copy-start(f32[1536,768]{0,1:T(8,128)} %all-reduce.5.cloned.1.call-done) | copy-start | bytes 14155780
  564.6 5.4 copy-start.5
  564.7 5.4 copy-start.10
  592.1 3.1 copy-start.12
  595.2 6.1 copy-start.6
  595.2 6.1 copy-start.9
  601.4 2.4 copy-start.3
  601.4 3.4 copy-start
  601.4 4.1 copy-start.1
  601.4 4.8 copy-start.2
  633.5 16.5 %copy-start.11 = (f32[384,384]{0,1:T(8,128)S(1)}, f32[384,384]{0,1:T(8,128)}, u32[]{:S(2)}) copy-start(f32[384,384]{0,1:T(8,128)} %get-tuple-element.48) | copy-start | bytes 1769476
  633.5 16.8 %copy-start.4 = (f32[384,4,384]{2,0,1:T(8,128)S(1)}, f32[384,4,384]{2,0,1:T(8,128)}, u32[]{:S(2)}) copy-start(f32[384,4,384]{2,0,1:T(8,128)} %copy-done.3) | copy-start | bytes 7077892
  650.2 1.7 copy-start.7
Sparse Core Ops, SparseCore 0:
  18.9 117.8 all-reduce.4
  178.8 174.6 all-reduce.6

commit v2 on v1

--- a/solution.py
+++ b/solution.py
@@ -2,8 +2,66 @@
 import jax.numpy as jnp
 from jax import lax
 from jax.sharding import PartitionSpec as P
+from jax.experimental import pallas as pl
+from jax.experimental.pallas import tpu as pltpu
 
 STEPS = 2
+
+TILE = 128
+GROUP = 8
+
+
+def _chol_inv_kernel(a_ref, u_ref, m_ref, w_ref):
+    n = a_ref.shape[0]
+    w_ref[...] = a_ref[...]
+    u_ref[...] = jnp.zeros_like(u_ref)
+    rows = lax.broadcasted_iota(jnp.int32, (n, n), 0)
+    cols = lax.broadcasted_iota(jnp.int32, (n, n), 1)
+    m_ref[...] = jnp.where(rows == cols, 1.0, 0.0).astype(jnp.float32)
+    for b in range(n // TILE):
+        lo = b * TILE
+        span = n - lo
+        done = lo + TILE
+
+        def group(q, carry, lo=lo, span=span, done=done):
+            base = pl.multiple_of(lo + q * GROUP, GROUP)
+            sub = lax.broadcasted_iota(jnp.int32, (GROUP, 1), 0)
+            lane = lax.broadcasted_iota(jnp.int32, (1, span), 1)
+            tlane = lax.broadcasted_iota(jnp.int32, (span, TILE), 1)
+            rid = lax.broadcasted_iota(jnp.int32, (span, 1), 0)
+            for r in range(GROUP):
+                kk = q * GROUP + r
+                a_row = w_ref[pl.ds(base, GROUP), pl.ds(lo, span)][r:r + 1, :]
+                pivot = jnp.sum(jnp.where(lane == kk, a_row, 0.0), axis=1, keepdims=True)
+                scale = 1.0 / jnp.sqrt(pivot)
+                u = jnp.where(lane >= kk, a_row * scale, 0.0)
+                u8 = u_ref[pl.ds(base, GROUP), pl.ds(lo, span)]
+                u_ref[pl.ds(base, GROUP), pl.ds(lo, span)] = jnp.where(sub == r, u, u8)
+                m8 = m_ref[pl.ds(base, GROUP), pl.ds(0, done)]
+                m_row = m8[r:r + 1, :] * scale
+                m_ref[pl.ds(base, GROUP), pl.ds(0, done)] = jnp.where(sub == r, m_row, m8)
+                tile = w_ref[pl.ds(lo, span), pl.ds(lo, TILE)]
+                ucol = jnp.sum(jnp.where(tlane == kk, tile, 0.0), axis=1, keepdims=True) * scale
+                ucol = jnp.where(rid > kk, ucol, 0.0)
+                w_ref[pl.ds(lo, span), pl.ds(lo, span)] = w_ref[pl.ds(lo, span), pl.ds(lo, span)] - ucol * u
+                m_ref[pl.ds(lo, span), pl.ds(0, done)] = m_ref[pl.ds(lo, span), pl.ds(0, done)] - ucol * m_row
+            return carry
+
+        lax.fori_loop(0, TILE // GROUP, group, 0)
+
+
+def chol_inv(a):
+    n = a.shape[0]
+    return pl.pallas_call(
+        _chol_inv_kernel,
+        out_shape=(jax.ShapeDtypeStruct((n, n), jnp.float32), jax.ShapeDtypeStruct((n, n), jnp.float32)),
+        scratch_shapes=[pltpu.VMEM((n, n), jnp.float32)],
+        cost_estimate=pl.CostEstimate(flops=2 * n * n * n, bytes_accessed=3 * n * n * 4, transcendentals=n),
+    )(a)
+
+
+def symmetric(a):
+    return (a + a.T) * jnp.float32(0.5)
 
 
 def shards(matrix):
@@ -13,7 +71,6 @@
     count = matrix.shape[1]
     width = matrix.shape[2]
     glob = jnp.arange(count, dtype=jnp.int32) * ncol + column
-    ident = jnp.eye(width, dtype=jnp.float32)
     own = matrix[:, 0, :]
     zero = jnp.zeros_like(own)
     both = lax.psum(
@@ -28,12 +85,10 @@
     g00 = gram[:width, :width]
     g10 = gram[width:, :width]
     g11 = gram[width:, width:]
-    lower0 = jnp.linalg.cholesky(g00)
-    inv0 = lax.linalg.triangular_solve(lower0, ident, left_side=True, lower=True)
+    upper0, inv0 = chol_inv(symmetric(g00))
     xmat = jnp.dot(g10, inv0.T, precision=highest, preferred_element_type=jnp.float32)
     schur = g11 - jnp.dot(xmat, xmat.T, precision=highest, preferred_element_type=jnp.float32)
-    lower1 = jnp.linalg.cholesky(schur)
-    inv1 = lax.linalg.triangular_solve(lower1, ident, left_side=True, lower=True)
+    upper1, inv1 = chol_inv(symmetric(schur))
     proj0 = jnp.einsum("ab,bjt->ajt", inv0, cross[:width], precision=highest)
     rest1 = cross[width:] - jnp.einsum("ab,bjt->ajt", xmat, proj0, precision=highest)
     proj1 = jnp.einsum("ab,bjt->ajt", inv1, rest1, precision=highest)
@@ -49,8 +104,8 @@
     blocks = matrix - jnp.einsum("mb,bjt->mjt", basis, kept, precision=highest)
     blocks = jnp.where((glob == 0)[None, :, None], basis0[:, None, :], blocks)
     blocks = jnp.where((glob == 1)[None, :, None], basis1[:, None, :], blocks)
-    row0 = jnp.where((glob == 0)[None, :, None], lower0.T[:, None, :], kept0)
-    row1 = jnp.where((glob == 1)[None, :, None], lower1.T[:, None, :], kept1)
+    row0 = jnp.where((glob == 0)[None, :, None], upper0[:, None, :], kept0)
+    row1 = jnp.where((glob == 1)[None, :, None], upper1[:, None, :], kept1)
     return (blocks, jnp.stack([row0, row1]))
 
 

time: 673 us -> 604 us (0.90)
  other arithmetic: 184 us -> 8.56 us
  Pallas kernels: 0 us -> 131 us
  local copies, waits for them, and re-layouts: 53.4 us -> 38.3 us
  matrix products: 116 us -> 109 us
    another operation x24 -> x0, other arithmetic: 173 us -> none  [the longest x11 57.1 us: shards(): lower1 = jnp.linalg.cholesky(schur)]
    pallas_call x0 -> x2, Pallas kernels: none -> 131 us  [chol_inv(): pl.pallas_call(_chol_inv_kernel, out_shape=(jax.ShapeDtypeStruct((n, n),...]
    another operation x27 -> x0, local copies, waits for them, and re-layouts: 12.4 us -> none  [the longest x12 6.25 us: shards(): lax.linalg.triangular_solve(lower0, ident, left_side=True, lower=True)]
    unnamed x29 -> x27, local copies, waits for them, and re-layouts: 31.2 us -> 29.6 us
where the time goes in v2:
time: 604 us; the launch traced here: 595 us
  waiting for transfers between devices  293 us (49%)
  Pallas kernels  131 us (22%)
  matrix products  109 us (18%)
  local copies, waits for them, and re-layouts  38.3 us (6%)
  between operations  14.7 us (2%)
  other arithmetic  8.56 us (1%)
    psum x1, waiting for transfers between devices, shards(): gram, cross = lax.psum((gram_part, cross_part), 'row')  175 us
    pallas_call x2, Pallas kernels, chol_inv(): pl.pallas_call(_chol_inv_kernel, out_shape=(jax.ShapeDtypeStruct((n, n),...  131 us
    psum x1, waiting for transfers between devices, shards(): lax.psum(jnp.concatenate([jnp.where(column == 0, own, zero), jnp.where(co...  118 us
    unnamed x27, local copies, waits for them, and re-layouts  29.6 us
    dot_general x1, matrix products, shards(): blocks = matrix - jnp.einsum('mb,bjt->mjt', basis, kept, precision=highest)  27.3 us
    dot_general x1, matrix products, shards(): cross_part = jnp.einsum('mb,mjt->bjt', both, matrix, precision=highest)  25.9 us
    dot_general x1, matrix products, shards(): jnp.dot(both.T, both, precision=highest, preferred_element_type=jnp.float32)  15.8 us
  transfers between devices with their start and end apart: 2, of which 2 were waited for; matrix products, arithmetic and copies ran while one was open for 0% of the time, Pallas kernels for 0%

profile of v2, /device:TPU:0, one launch (start us, length us, event | category | flops | bytes accessed | tf_op | source)
XLA Modules:
  0.0 594.9 jit_solution(5003422946618745656)
XLA Ops:
  7.2 1.7 slice-done
  8.9 5.1 copy.20
  14.0 2.2 select_bitcast_fusion.3
  16.2 2.5 pad_maximum_fusion
  18.8 118.0 %all-reduce.4.cloned.1.call-done = f32[1536,768]{0,1:T(8,128)} async-done(((f32[1536,768]{0,1:T(8,128)}), f32[1536,768]{0,1:T(8,128)}) %all-reduce.4.cloned.1.call-update) | async-done | bytes 4718608 | tf_op jit(solution)/shard_map/psum | solution.py:76
  136.8 15.8 %fusion.22 = f32[768,768]{0,1:T(8,128)} fusion(f32[1536,768]{0,1:T(8,128)} %all-reduce.4.cloned.1.call-done), kind=kOutput, calls=%fused_computation.42 | convolution fusion | flops 10871635968 | bytes 7077888 | tf_op jit(solution)/shard_map/dot_general | solution.py:82
  152.6 25.9 %fusion = f32[768,4,384]{2,0,1:T(8,128)} fusion(f32[1536,4,384]{2,1,0:T(4,128)} %param.1, f32[1536,768]{0,1:T(8,128)S(1)} %copy-done.6), kind=kOutput, calls=%fused_computation.1 | convolution fusion | flops 21743271936 | bytes 18874368 | tf_op jit(solution)/shard_map/mb,mjt->bjt/dot_general | solution.py:83
  178.5 175.0 %all-reduce.6.cloned.1.call-done = (f32[768,768]{0,1:T(8,128)}, f32[768,4,384]{2,0,1:T(8,128)}) async-done(((f32[768,768]{0,1:T(8,128)}, f32[768,4,384]{2,0,1:T(8,128)}), (f32[768,768]{0,1:T(8,128)}, f32[768,4,384]{2,0,1:T(8,128)})) %all-reduce.6.cloned.1.call-update) | async-done | bytes 7077904 | tf_op jit(solution)/shard_map/psum | solution.py:84
  353.5 1.1 slice.34
  354.9 1.9 fusion.20.a_ref
  356.8 65.7 %shard_map.30 = (f32[384,384]{1,0:T(8,128)}, f32[384,384]{1,0:T(8,128)}) custom-call(f32[384,384]{1,0:T(8,128)} %fusion.20.a_ref), custom_call_target="tpu_custom_call" | custom-call | flops 113246208 | bytes 1769472 | tf_op jit(solution)/shard_map/pallas_call | solution.py:55
  422.5 3.3 fusion.14
  425.8 2.3 convolution_subtract_fusion.1
  428.7 0.9 broadcast_multiply_fusion.a_ref
  429.6 65.6 %shard_map.31 = (f32[384,384]{1,0:T(8,128)}, f32[384,384]{1,0:T(8,128)}) custom-call(f32[384,384]{1,0:T(8,128)} %broadcast_multiply_fusion.a_ref), custom_call_target="tpu_custom_call" | custom-call | flops 113246208 | bytes 1769472 | tf_op jit(solution)/shard_map/pallas_call | solution.py:55
  495.2 5.7 fusion.9
  500.9 5.4 fusion.16
  506.3 5.3 fusion.11
  511.6 2.2 copy.10
  513.9 6.5 %convolution_subtract_fusion = f32[1536,384]{0,1:T(8,128)S(1)} fusion(f32[1536,384]{0,1:T(8,128)} %fusion.11, f32[384,384]{1,0:T(8,128)S(1)} %fusion.14, f32[1536,768]{0,1:T(8,128)} %all-reduce.4.cloned.1.call-done), kind=kOutput, calls=%fused_computation.12 | convolution fusion | flops 2718498816 | bytes 7667712 | tf_op jit(solution)/shard_map/dot_general | solution.py:98
  520.4 5.4 fusion.23
  525.7 3.1 copy.9
  528.8 6.1 %fusion.13 = f32[384,4,384]{2,0,1:T(8,128)S(1)} fusion(f32[384,4,384]{2,0,1:T(8,128)} %fusion.16, f32[768,4,384]{2,0,1:T(8,128)} %get-tuple-element.13, pred[4]{0:T(512)(128)(4,1)S(1)} %get-tuple-element.19, f32[384,384]{1,0:T(8,128)S(1)} %copy-done.7), kind=kOutput, calls=%fused_computation.23 | convolution fusion | flops 2719088640 | bytes 7667716 | tf_op jit(solution)/shard_map/ab,bjt->ajt/dot_general | solution.py:94
  535.0 0.4 select_bitcast_fusion.1
  535.4 1.2 copy-done
  536.6 0.7 copy-done.1
  537.3 0.7 copy-done.2
  538.0 27.3 %select_select_fusion = f32[1536,4,384]{2,0,1:T(8,128)S(1)} fusion(f32[1536,4,384]{2,1,0:T(4,128)} %param.1, f32[1536,384]{0,1:T(8,128)S(1)} %copy-done.2, f32[1536,384]{0,1:T(8,128)S(1)} %copy-done.1, f32[384,4,384]{2,0,1:T(8,128)S(1)} %fusion.13, f32[384,4,384]{2,0,1:T(8,128)S(1)} %get-tuple-element.15, f32[1536,384]{1,0:T(8,128)S(1)} %copy.10, ...), kind=kOutput, calls=%fused_computation | convolution fusion | flops 21752709120 | bytes 33030152 | tf_op jit(solution)/shard_map/mb,bjt->mjt/dot_general | solution.py:104
  565.3 16.5 %copy.14 = f32[1536,4,384]{2,1,0:T(4,128)} copy(f32[1536,4,384]{2,0,1:T(8,128)S(1)} %select_select_fusion) | data formatting | bytes 18874368
  581.9 0.2 select_bitcast_fusion
  582.1 0.3 pad_maximum_fusion.1
  582.4 5.2 copy.15
  (34 shorter events, 0.9 us)
Async XLA Ops:
  7.2 129.6 %all-reduce.4.cloned.1.call-start = ((), (), s32[]{:S(2)}) async-start(), calls=%async_computation | async-start | bytes 9437184 | tf_op jit(solution)/shard_map/psum | solution.py:76
  7.2 1.7 slice-start
  18.8 334.8 %all-reduce.6.cloned.1.call-start = ((), (), s32[]{:S(2)}) async-start(), calls=%async_computation.1 | async-start | bytes 14155776 | tf_op jit(solution)/shard_map/psum | solution.py:84
  136.8 15.8 %copy-start.6 = (f32[1536,768]{0,1:T(8,128)S(1)}, f32[1536,768]{0,1:T(8,128)}, u32[]{:S(2)}) copy-start(f32[1536,768]{0,1:T(8,128)} %all-reduce.4.cloned.1.call-done) | copy-start | bytes 14155780
  428.4 66.8 %copy-start.5 = (f32[384,384]{1,0:T(8,128)S(1)}, f32[384,384]{1,0:T(8,128)}, u32[]{:S(2)}) copy-start(f32[384,384]{1,0:T(8,128)} %get-tuple-element.6) | copy-start | bytes 1769476
  428.7 77.6 %slice-start.1 = ((s8[4718592]{0:T(1024)(128)(4,1)}), s8[524288]{0:T(1024)(128)(4,1)S(1)}, s32[]{:S(2)}) async-start(s8[4718592]{0:T(1024)(128)(4,1)} %bitcast.40), calls=%async_computation.3 | async-start | bytes 1048576
  495.2 11.1 %slice-start.2 = ((s8[4718592]{0:T(1024)(128)(4,1)}), s8[4194304]{0:T(1024)(128)(4,1)S(1)}, s32[]{:S(2)}) async-start(s8[4718592]{0:T(1024)(128)(4,1)} %bitcast.40), calls=%async_computation.4 | async-start | bytes 8388608
  500.9 5.4 copy-start.3
  513.9 6.5 %copy-start.7 = (f32[384,384]{1,0:T(8,128)S(1)}, f32[384,384]{1,0:T(8,128)}, u32[]{:S(2)}) copy-start(f32[384,384]{1,0:T(8,128)} %get-tuple-element.7) | copy-start | bytes 1769476
  528.8 6.1 %copy-start.4 = (f32[384,4,384]{2,0,1:T(8,128)S(1)}, f32[384,4,384]{2,0,1:T(8,128)}, u32[]{:S(2)}) copy-start(f32[384,4,384]{2,0,1:T(8,128)} %copy-done.3) | copy-start | bytes 7077892
  528.8 6.1 %copy-start.8 = (f32[384,384]{1,0:T(8,128)S(1)}, f32[384,384]{1,0:T(8,128)}, u32[]{:S(2)}) copy-start(f32[384,384]{1,0:T(8,128)} %get-tuple-element.8) | copy-start | bytes 1769476
  534.9 1.7 copy-start
  535.0 2.4 copy-start.1
  535.0 3.1 copy-start.2
  565.3 16.5 %copy-start.9 = (f32[384,384]{1,0:T(8,128)S(1)}, f32[384,384]{1,0:T(8,128)}, u32[]{:S(2)}) copy-start(f32[384,384]{1,0:T(8,128)} %get-tuple-element.9) | copy-start | bytes 1769476
Sparse Core Ops, SparseCore 0:
  18.9 117.8 all-reduce.3
  178.6 174.8 all-reduce.5

commit v3 on v2

--- a/solution.py
+++ b/solution.py
@@ -80,7 +80,7 @@
         "col",
     )
     gram_part = jnp.dot(both.T, both, precision=highest, preferred_element_type=jnp.float32)
-    cross_part = jnp.einsum("mb,mjt->bjt", both, matrix, precision=highest)
+    cross_part = jnp.einsum("mb,mjt->bjt", both, matrix, precision=lax.Precision.HIGH)
     gram, cross = lax.psum((gram_part, cross_part), "row")
     g00 = gram[:width, :width]
     g10 = gram[width:, :width]
@@ -101,7 +101,7 @@
     kept1 = jnp.where((glob > 1)[None, :, None], proj1, jnp.float32(0.0))
     basis = jnp.concatenate([basis0, basis1], axis=1)
     kept = jnp.concatenate([kept0, kept1], axis=0)
-    blocks = matrix - jnp.einsum("mb,bjt->mjt", basis, kept, precision=highest)
+    blocks = matrix - jnp.einsum("mb,bjt->mjt", basis, kept, precision=lax.Precision.HIGH)
     blocks = jnp.where((glob == 0)[None, :, None], basis0[:, None, :], blocks)
     blocks = jnp.where((glob == 1)[None, :, None], basis1[:, None, :], blocks)
     row0 = jnp.where((glob == 0)[None, :, None], upper0[:, None, :], kept0)

time: 604 us -> 589 us (0.975)
  matrix products: 109 us -> 92.3 us
    dot_general x2, matrix products: 53.2 us -> 34.9 us  [the longest x1 19.8 us: shards(): jnp.einsum('mb,bjt->mjt', basis, kept, precision=lax.Precision.HIGH)]
    unnamed x27 -> x29, local copies, waits for them, and re-layouts: 29.6 us -> 30.6 us
where the time goes in v3:
time: 589 us; the launch traced here: 582 us
  waiting for transfers between devices  293 us (50%)
  Pallas kernels  131 us (22%)
  matrix products  92.3 us (16%)
  local copies, waits for them, and re-layouts  39.4 us (7%)
  between operations  14.7 us (2%)
  other arithmetic  11 us (2%)
    psum x1, waiting for transfers between devices, shards(): gram, cross = lax.psum((gram_part, cross_part), 'row')  175 us
    pallas_call x2, Pallas kernels, chol_inv(): pl.pallas_call(_chol_inv_kernel, out_shape=(jax.ShapeDtypeStruct((n, n),...  131 us
    psum x1, waiting for transfers between devices, shards(): lax.psum(jnp.concatenate([jnp.where(column == 0, own, zero), jnp.where(co...  118 us
    unnamed x29, local copies, waits for them, and re-layouts  30.6 us
    dot_general x1, matrix products, shards(): jnp.einsum('mb,bjt->mjt', basis, kept, precision=lax.Precision.HIGH)  19.8 us
    dot_general x1, matrix products, shards(): jnp.dot(both.T, both, precision=highest, preferred_element_type=jnp.float32)  15.8 us
    dot_general x1, matrix products, shards(): jnp.einsum('mb,mjt->bjt', both, matrix, precision=lax.Precision.HIGH)  15.1 us
  transfers between devices with their start and end apart: 2, of which 2 were waited for; matrix products, arithmetic and copies ran while one was open for 0% of the time, Pallas kernels for 0%

profile of v3, /device:TPU:0, one launch (start us, length us, event | category | flops | bytes accessed | tf_op | source)
XLA Modules:
  0.0 581.6 jit_solution(2079298105101910606)
XLA Ops:
  7.2 1.7 slice-done
  8.9 5.1 copy.20
  14.0 2.2 select_bitcast_fusion.3
  16.2 2.5 pad_maximum_fusion
  18.8 118.0 %all-reduce.4.cloned.1.call-done = f32[1536,768]{0,1:T(8,128)} async-done(((f32[1536,768]{0,1:T(8,128)}), f32[1536,768]{0,1:T(8,128)}) %all-reduce.4.cloned.1.call-update) | async-done | bytes 4718608 | tf_op jit(solution)/shard_map/psum | solution.py:76
  136.8 15.8 %fusion.22 = f32[768,768]{0,1:T(8,128)} fusion(f32[1536,768]{0,1:T(8,128)} %all-reduce.4.cloned.1.call-done), kind=kOutput, calls=%fused_computation.42 | convolution fusion | flops 10871635968 | bytes 7077888 | tf_op jit(solution)/shard_map/dot_general | solution.py:82
  152.6 15.1 %fusion = f32[768,4,384]{2,0,1:T(8,128)} fusion(f32[1536,4,384]{2,1,0:T(4,128)} %param.1, f32[1536,768]{0,1:T(8,128)S(1)} %copy-done.7), kind=kOutput, calls=%fused_computation.1 | convolution fusion | flops 10871635968 | bytes 18874368 | tf_op jit(solution)/shard_map/mb,mjt->bjt/dot_general | solution.py:83
  167.7 174.8 %all-reduce.6.cloned.1.call-done = (f32[768,768]{0,1:T(8,128)}, f32[768,4,384]{2,0,1:T(8,128)}) async-done(((f32[768,768]{0,1:T(8,128)}, f32[768,4,384]{2,0,1:T(8,128)}), (f32[768,768]{0,1:T(8,128)}, f32[768,4,384]{2,0,1:T(8,128)})) %all-reduce.6.cloned.1.call-update) | async-done | bytes 7077904 | tf_op jit(solution)/shard_map/psum | solution.py:84
  342.5 1.1 slice.34
  343.8 1.9 fusion.20.a_ref
  345.7 65.9 %shard_map.30 = (f32[384,384]{1,0:T(8,128)}, f32[384,384]{1,0:T(8,128)}) custom-call(f32[384,384]{1,0:T(8,128)} %fusion.20.a_ref), custom_call_target="tpu_custom_call" | custom-call | flops 113246208 | bytes 1769472 | tf_op jit(solution)/shard_map/pallas_call | solution.py:55
  411.6 3.3 fusion.14
  414.9 2.3 convolution_subtract_fusion.1
  417.2 0.2 copy.7
  417.8 0.9 broadcast_multiply_fusion.a_ref
  418.6 65.6 %shard_map.31 = (f32[384,384]{1,0:T(8,128)}, f32[384,384]{1,0:T(8,128)}) custom-call(f32[384,384]{1,0:T(8,128)} %broadcast_multiply_fusion.a_ref), custom_call_target="tpu_custom_call" | custom-call | flops 113246208 | bytes 1769472 | tf_op jit(solution)/shard_map/pallas_call | solution.py:55
  484.3 5.7 fusion.9
  490.0 5.3 fusion.16
  495.3 5.3 fusion.11
  500.7 2.2 copy.10
  502.9 6.5 %convolution_subtract_fusion = f32[1536,384]{0,1:T(8,128)S(1)} fusion(f32[1536,384]{0,1:T(8,128)} %fusion.11, f32[384,384]{1,0:T(8,128)S(1)} %fusion.14, f32[1536,768]{0,1:T(8,128)} %all-reduce.4.cloned.1.call-done), kind=kOutput, calls=%fused_computation.12 | convolution fusion | flops 2718498816 | bytes 7667712 | tf_op jit(solution)/shard_map/dot_general | solution.py:98
  509.4 5.4 fusion.23
  514.8 3.1 copy.9
  517.9 7.8 %fusion.13 = f32[384,4,384]{2,0,1:T(8,128)} fusion(f32[384,4,384]{2,0,1:T(8,128)} %fusion.16, f32[768,4,384]{2,0,1:T(8,128)} %get-tuple-element.13, pred[4]{0:T(512)(128)(4,1)S(1)} %get-tuple-element.19, f32[384,384]{1,0:T(8,128)S(1)} %copy-done.8), kind=kOutput, calls=%fused_computation.23 | convolution fusion | flops 2719088640 | bytes 7667716 | tf_op jit(solution)/shard_map/ab,bjt->ajt/dot_general | solution.py:94
  525.7 2.8 select_bitcast_fusion.1
  528.5 1.3 copy-done.1
  529.8 19.8 %select_select_fusion = f32[1536,4,384]{2,0,1:T(8,128)} fusion(f32[1536,4,384]{2,1,0:T(4,128)} %param.1, f32[1536,384]{0,1:T(8,128)} %fusion.23, f32[1536,384]{0,1:T(8,128)S(1)} %copy-done.1, f32[384,4,384]{2,0,1:T(8,128)} %fusion.13, f32[384,4,384]{2,0,1:T(8,128)} %get-tuple-element.15, f32[1536,384]{1,0:T(8,128)S(1)} %copy.10, f32[1536,384]{1,0:T(8,128)S(1)} %copy-done, ...), kind=kOutput, calls=%fused_computation | convolution fusion | flops 10881073152 | bytes 33030152 | tf_op jit(solution)/shard_map/mb,bjt->mjt/dot_general | solution.py:104
  549.6 17.5 %copy.14 = f32[1536,4,384]{2,1,0:T(4,128)} copy(f32[1536,4,384]{2,0,1:T(8,128)} %select_select_fusion) | data formatting | bytes 18874368
  567.1 0.2 select_bitcast_fusion
  567.4 1.4 copy-done.5
  568.8 0.3 pad_maximum_fusion.1
  569.1 5.2 copy.15
  (36 shorter events, 0.7 us)
Async XLA Ops:
  7.2 129.6 %all-reduce.4.cloned.1.call-start = ((), (), s32[]{:S(2)}) async-start(), calls=%async_computation | async-start | bytes 9437184 | tf_op jit(solution)/shard_map/psum | solution.py:76
  7.2 1.7 slice-start
  18.8 323.7 %all-reduce.6.cloned.1.call-start = ((), (), s32[]{:S(2)}) async-start(), calls=%async_computation.1 | async-start | bytes 14155776 | tf_op jit(solution)/shard_map/psum | solution.py:84
  136.8 15.8 %copy-start.7 = (f32[1536,768]{0,1:T(8,128)S(1)}, f32[1536,768]{0,1:T(8,128)}, u32[]{:S(2)}) copy-start(f32[1536,768]{0,1:T(8,128)} %all-reduce.4.cloned.1.call-done) | copy-start | bytes 14155780
  417.5 66.8 %copy-start.6 = (f32[384,384]{1,0:T(8,128)S(1)}, f32[384,384]{1,0:T(8,128)}, u32[]{:S(2)}) copy-start(f32[384,384]{1,0:T(8,128)} %get-tuple-element.6) | copy-start | bytes 1769476
  417.8 77.5 %slice-start.1 = ((s8[4718592]{0:T(1024)(128)(4,1)}), s8[524288]{0:T(1024)(128)(4,1)S(1)}, s32[]{:S(2)}) async-start(s8[4718592]{0:T(1024)(128)(4,1)} %bitcast.40), calls=%async_computation.3 | async-start | bytes 1048576
  484.3 11.1 %slice-start.2 = ((s8[4718592]{0:T(1024)(128)(4,1)}), s8[4194304]{0:T(1024)(128)(4,1)S(1)}, s32[]{:S(2)}) async-start(s8[4718592]{0:T(1024)(128)(4,1)} %bitcast.40), calls=%async_computation.4 | async-start | bytes 8388608
  490.0 5.3 copy-start.3
  502.9 6.5 %copy-start.8 = (f32[384,384]{1,0:T(8,128)S(1)}, f32[384,384]{1,0:T(8,128)}, u32[]{:S(2)}) copy-start(f32[384,384]{1,0:T(8,128)} %get-tuple-element.7) | copy-start | bytes 1769476
  517.9 7.8 %copy-start.4 = (f32[384,4,384]{2,0,1:T(8,128)S(1)}, f32[384,4,384]{2,0,1:T(8,128)}, u32[]{:S(2)}) copy-start(f32[384,4,384]{2,0,1:T(8,128)} %copy-done.3) | copy-start | bytes 7077892
  517.9 7.8 %copy-start.9 = (f32[384,384]{1,0:T(8,128)S(1)}, f32[384,384]{1,0:T(8,128)}, u32[]{:S(2)}) copy-start(f32[384,384]{1,0:T(8,128)} %get-tuple-element.8) | copy-start | bytes 1769476
  525.7 2.8 copy-start
  525.7 4.1 copy-start.1
  549.6 17.6 %copy-start.2 = (f32[384,4,384]{2,0,1:T(8,128)S(1)}, f32[384,4,384]{2,0,1:T(8,128)}, u32[]{:S(2)}) copy-start(f32[384,4,384]{2,0,1:T(8,128)} %fusion.13) | copy-start | bytes 7077892
  549.6 17.6 %copy-start.10 = (f32[384,384]{1,0:T(8,128)S(1)}, f32[384,384]{1,0:T(8,128)}, u32[]{:S(2)}) copy-start(f32[384,384]{1,0:T(8,128)} %get-tuple-element.9) | copy-start | bytes 1769476
  567.1 1.7 copy-start.5
Sparse Core Ops, SparseCore 0:
  18.9 117.8 all-reduce.3
  167.8 174.6 all-reduce.5

commit v4 on v3

--- a/solution.py
+++ b/solution.py
@@ -11,43 +11,64 @@
 GROUP = 8
 
 
-def _chol_inv_kernel(a_ref, u_ref, m_ref, w_ref):
+def _mm(a, b):
+    return jnp.dot(a, b, precision=lax.Precision.HIGHEST, preferred_element_type=jnp.float32)
+
+
+def _chol_inv_kernel(a_ref, u_ref, m_ref, w_ref, t_ref, d_ref, e_ref):
     n = a_ref.shape[0]
+    nb = n // TILE
     w_ref[...] = a_ref[...]
     u_ref[...] = jnp.zeros_like(u_ref)
-    rows = lax.broadcasted_iota(jnp.int32, (n, n), 0)
-    cols = lax.broadcasted_iota(jnp.int32, (n, n), 1)
-    m_ref[...] = jnp.where(rows == cols, 1.0, 0.0).astype(jnp.float32)
-    for b in range(n // TILE):
+    m_ref[...] = jnp.zeros_like(m_ref)
+    rows = lax.broadcasted_iota(jnp.int32, (TILE, TILE), 0)
+    cols = lax.broadcasted_iota(jnp.int32, (TILE, TILE), 1)
+    eye = jnp.where(rows == cols, 1.0, 0.0).astype(jnp.float32)
+    sub = lax.broadcasted_iota(jnp.int32, (GROUP, 1), 0)
+    lane = lax.broadcasted_iota(jnp.int32, (1, TILE), 1)
+    rid = lax.broadcasted_iota(jnp.int32, (TILE, 1), 0)
+    for b in range(nb):
         lo = b * TILE
-        span = n - lo
-        done = lo + TILE
+        hi = lo + TILE
+        t_ref[...] = w_ref[lo:hi, lo:hi]
+        d_ref[...] = eye
+        e_ref[...] = jnp.zeros_like(e_ref)
 
-        def group(q, carry, lo=lo, span=span, done=done):
-            base = pl.multiple_of(lo + q * GROUP, GROUP)
-            sub = lax.broadcasted_iota(jnp.int32, (GROUP, 1), 0)
-            lane = lax.broadcasted_iota(jnp.int32, (1, span), 1)
-            tlane = lax.broadcasted_iota(jnp.int32, (span, TILE), 1)
-            rid = lax.broadcasted_iota(jnp.int32, (span, 1), 0)
+        def group(q, carry):
+            base = pl.multiple_of(q * GROUP, GROUP)
             for r in range(GROUP):
                 kk = q * GROUP + r
-                a_row = w_ref[pl.ds(base, GROUP), pl.ds(lo, span)][r:r + 1, :]
+                a_row = t_ref[pl.ds(base, GROUP), :][r:r + 1, :]
                 pivot = jnp.sum(jnp.where(lane == kk, a_row, 0.0), axis=1, keepdims=True)
                 scale = 1.0 / jnp.sqrt(pivot)
                 u = jnp.where(lane >= kk, a_row * scale, 0.0)
-                u8 = u_ref[pl.ds(base, GROUP), pl.ds(lo, span)]
-                u_ref[pl.ds(base, GROUP), pl.ds(lo, span)] = jnp.where(sub == r, u, u8)
-                m8 = m_ref[pl.ds(base, GROUP), pl.ds(0, done)]
+                u8 = e_ref[pl.ds(base, GROUP), :]
+                e_ref[pl.ds(base, GROUP), :] = jnp.where(sub == r, u, u8)
+                m8 = d_ref[pl.ds(base, GROUP), :]
                 m_row = m8[r:r + 1, :] * scale
-                m_ref[pl.ds(base, GROUP), pl.ds(0, done)] = jnp.where(sub == r, m_row, m8)
-                tile = w_ref[pl.ds(lo, span), pl.ds(lo, TILE)]
-                ucol = jnp.sum(jnp.where(tlane == kk, tile, 0.0), axis=1, keepdims=True) * scale
+                d_ref[pl.ds(base, GROUP), :] = jnp.where(sub == r, m_row, m8)
+                tile = t_ref[...]
+                ucol = jnp.sum(jnp.where(cols == kk, tile, 0.0), axis=1, keepdims=True) * scale
                 ucol = jnp.where(rid > kk, ucol, 0.0)
-                w_ref[pl.ds(lo, span), pl.ds(lo, span)] = w_ref[pl.ds(lo, span), pl.ds(lo, span)] - ucol * u
-                m_ref[pl.ds(lo, span), pl.ds(0, done)] = m_ref[pl.ds(lo, span), pl.ds(0, done)] - ucol * m_row
+                t_ref[...] = tile - ucol * u
+                d_ref[...] = d_ref[...] - ucol * m_row
             return carry
 
         lax.fori_loop(0, TILE // GROUP, group, 0)
+        u_ref[lo:hi, lo:hi] = e_ref[...]
+        m_ref[lo:hi, lo:hi] = d_ref[...]
+        if b + 1 < nb:
+            panel = _mm(d_ref[...], w_ref[lo:hi, hi:n])
+            u_ref[lo:hi, hi:n] = panel
+            w_ref[hi:n, hi:n] = w_ref[hi:n, hi:n] - _mm(panel.T, panel)
+    for i in range(1, nb):
+        di = m_ref[i * TILE:(i + 1) * TILE, i * TILE:(i + 1) * TILE]
+        for j in range(i - 1, -1, -1):
+            acc = jnp.zeros((TILE, TILE), jnp.float32)
+            for k in range(j, i):
+                low_ik = u_ref[k * TILE:(k + 1) * TILE, i * TILE:(i + 1) * TILE].T
+                acc = acc + _mm(low_ik, m_ref[k * TILE:(k + 1) * TILE, j * TILE:(j + 1) * TILE])
+            m_ref[i * TILE:(i + 1) * TILE, j * TILE:(j + 1) * TILE] = -_mm(di, acc)
 
 
 def chol_inv(a):
@@ -55,7 +76,12 @@
     return pl.pallas_call(
         _chol_inv_kernel,
         out_shape=(jax.ShapeDtypeStruct((n, n), jnp.float32), jax.ShapeDtypeStruct((n, n), jnp.float32)),
-        scratch_shapes=[pltpu.VMEM((n, n), jnp.float32)],
+        scratch_shapes=[
+            pltpu.VMEM((n, n), jnp.float32),
+            pltpu.VMEM((TILE, TILE), jnp.float32),
+            pltpu.VMEM((TILE, TILE), jnp.float32),
+            pltpu.VMEM((TILE, TILE), jnp.float32),
+        ],
         cost_estimate=pl.CostEstimate(flops=2 * n * n * n, bytes_accessed=3 * n * n * 4, transcendentals=n),
     )(a)
 

time: 589 us -> 553 us (0.939)
  Pallas kernels: 131 us -> 96.1 us
    pallas_call x2, Pallas kernels: 131 us -> 96.1 us  [chol_inv(): pl.pallas_call(_chol_inv_kernel, out_shape=(jax.ShapeDtypeStruct((n, n),...]
where the time goes in v4:
time: 553 us; the launch traced here: 546 us
  waiting for transfers between devices  293 us (53%)
  Pallas kernels  96.1 us (17%)
  matrix products  92.3 us (17%)
  local copies, waits for them, and re-layouts  39.4 us (7%)
  between operations  14.7 us (3%)
  other arithmetic  11 us (2%)
    psum x1, waiting for transfers between devices, shards(): gram, cross = lax.psum((gram_part, cross_part), 'row')  175 us
    psum x1, waiting for transfers between devices, shards(): lax.psum(jnp.concatenate([jnp.where(column == 0, own, zero), jnp.where(co...  118 us
    pallas_call x2, Pallas kernels, chol_inv(): pl.pallas_call(_chol_inv_kernel, out_shape=(jax.ShapeDtypeStruct((n, n),...  96.1 us
    unnamed x29, local copies, waits for them, and re-layouts  30.6 us
    dot_general x1, matrix products, shards(): jnp.einsum('mb,bjt->mjt', basis, kept, precision=lax.Precision.HIGH)  19.8 us
    dot_general x1, matrix products, shards(): jnp.dot(both.T, both, precision=highest, preferred_element_type=jnp.float32)  15.8 us
    dot_general x1, matrix products, shards(): jnp.einsum('mb,mjt->bjt', both, matrix, precision=lax.Precision.HIGH)  15.1 us
  transfers between devices with their start and end apart: 2, of which 2 were waited for; matrix products, arithmetic and copies ran while one was open for 0% of the time, Pallas kernels for 0%

profile of v4, /device:TPU:0, one launch (start us, length us, event | category | flops | bytes accessed | tf_op | source)
XLA Modules:
  0.0 546.2 jit_solution(2070866515241648462)
XLA Ops:
  7.2 1.7 slice-done
  8.9 5.1 copy.20
  14.0 2.2 select_bitcast_fusion.3
  16.2 2.5 pad_maximum_fusion
  18.8 118.0 %all-reduce.4.cloned.1.call-done = f32[1536,768]{0,1:T(8,128)} async-done(((f32[1536,768]{0,1:T(8,128)}), f32[1536,768]{0,1:T(8,128)}) %all-reduce.4.cloned.1.call-update) | async-done | bytes 4718608 | tf_op jit(solution)/shard_map/psum | solution.py:102
  136.8 15.8 %fusion.22 = f32[768,768]{0,1:T(8,128)} fusion(f32[1536,768]{0,1:T(8,128)} %all-reduce.4.cloned.1.call-done), kind=kOutput, calls=%fused_computation.42 | convolution fusion | flops 10871635968 | bytes 7077888 | tf_op jit(solution)/shard_map/dot_general | solution.py:108
  152.6 15.1 %fusion = f32[768,4,384]{2,0,1:T(8,128)} fusion(f32[1536,4,384]{2,1,0:T(4,128)} %param.1, f32[1536,768]{0,1:T(8,128)S(1)} %copy-done.7), kind=kOutput, calls=%fused_computation.1 | convolution fusion | flops 10871635968 | bytes 18874368 | tf_op jit(solution)/shard_map/mb,mjt->bjt/dot_general | solution.py:109
  167.7 174.8 %all-reduce.6.cloned.1.call-done = (f32[768,768]{0,1:T(8,128)}, f32[768,4,384]{2,0,1:T(8,128)}) async-done(((f32[768,768]{0,1:T(8,128)}, f32[768,4,384]{2,0,1:T(8,128)}), (f32[768,768]{0,1:T(8,128)}, f32[768,4,384]{2,0,1:T(8,128)})) %all-reduce.6.cloned.1.call-update) | async-done | bytes 7077904 | tf_op jit(solution)/shard_map/psum | solution.py:110
  342.5 1.1 slice.34
  343.6 0.2 copy.5
  343.8 1.9 fusion.20.a_ref
  345.7 48.2 %shard_map.30 = (f32[384,384]{1,0:T(8,128)}, f32[384,384]{1,0:T(8,128)}) custom-call(f32[384,384]{1,0:T(8,128)} %fusion.20.a_ref), custom_call_target="tpu_custom_call" | custom-call | flops 113246208 | bytes 1769472 | tf_op jit(solution)/shard_map/pallas_call | solution.py:76
  393.9 3.3 fusion.14
  397.2 2.3 convolution_subtract_fusion.1
  400.1 0.9 broadcast_multiply_fusion.a_ref
  400.9 47.9 %shard_map.31 = (f32[384,384]{1,0:T(8,128)}, f32[384,384]{1,0:T(8,128)}) custom-call(f32[384,384]{1,0:T(8,128)} %broadcast_multiply_fusion.a_ref), custom_call_target="tpu_custom_call" | custom-call | flops 113246208 | bytes 1769472 | tf_op jit(solution)/shard_map/pallas_call | solution.py:76
  448.9 5.7 %fusion.9 = f32[384,4,384]{2,0,1:T(8,128)S(1)} fusion(f32[768,4,384]{2,0,1:T(8,128)} %get-tuple-element.13, f32[384,384]{1,0:T(8,128)S(1)} %copy-done.6), kind=kOutput, calls=%fused_computation.15 | convolution fusion | flops 2717908992 | bytes 5308416 | tf_op jit(solution)/shard_map/ab,bjt->ajt/dot_general | solution.py:118
  454.6 5.3 fusion.16
  459.9 5.3 fusion.11
  465.3 2.2 copy.10
  467.5 6.5 %convolution_subtract_fusion = f32[1536,384]{0,1:T(8,128)S(1)} fusion(f32[1536,384]{0,1:T(8,128)} %fusion.11, f32[384,384]{1,0:T(8,128)S(1)} %fusion.14, f32[1536,768]{0,1:T(8,128)} %all-reduce.4.cloned.1.call-done), kind=kOutput, calls=%fused_computation.12 | convolution fusion | flops 2718498816 | bytes 7667712 | tf_op jit(solution)/shard_map/dot_general | solution.py:124
  474.0 5.4 fusion.23
  479.4 3.1 copy.9
  482.5 7.8 %fusion.13 = f32[384,4,384]{2,0,1:T(8,128)} fusion(f32[384,4,384]{2,0,1:T(8,128)} %fusion.16, f32[768,4,384]{2,0,1:T(8,128)} %get-tuple-element.13, pred[4]{0:T(512)(128)(4,1)S(1)} %get-tuple-element.19, f32[384,384]{1,0:T(8,128)S(1)} %copy-done.8), kind=kOutput, calls=%fused_computation.23 | convolution fusion | flops 2719088640 | bytes 7667716 | tf_op jit(solution)/shard_map/ab,bjt->ajt/dot_general | solution.py:120
  490.3 2.8 select_bitcast_fusion.1
  493.1 1.3 copy-done.1
  494.4 19.8 %select_select_fusion = f32[1536,4,384]{2,0,1:T(8,128)} fusion(f32[1536,4,384]{2,1,0:T(4,128)} %param.1, f32[1536,384]{0,1:T(8,128)} %fusion.23, f32[1536,384]{0,1:T(8,128)S(1)} %copy-done.1, f32[384,4,384]{2,0,1:T(8,128)} %fusion.13, f32[384,4,384]{2,0,1:T(8,128)} %get-tuple-element.15, f32[1536,384]{1,0:T(8,128)S(1)} %copy.10, f32[1536,384]{1,0:T(8,128)S(1)} %copy-done, ...), kind=kOutput, calls=%fused_computation | convolution fusion | flops 10881073152 | bytes 33030152 | tf_op jit(solution)/shard_map/mb,bjt->mjt/dot_general | solution.py:130
  514.2 17.5 %copy.14 = f32[1536,4,384]{2,1,0:T(4,128)} copy(f32[1536,4,384]{2,0,1:T(8,128)} %select_select_fusion) | data formatting | bytes 18874368
  531.7 0.2 select_bitcast_fusion
  532.0 1.4 copy-done.5
  533.4 0.3 pad_maximum_fusion.1
  533.7 5.2 copy.15
  (36 shorter events, 0.7 us)
Async XLA Ops:
  7.2 129.6 %all-reduce.4.cloned.1.call-start = ((), (), s32[]{:S(2)}) async-start(), calls=%async_computation | async-start | bytes 9437184 | tf_op jit(solution)/shard_map/psum | solution.py:102
  7.2 1.7 slice-start
  18.8 323.7 %all-reduce.6.cloned.1.call-start = ((), (), s32[]{:S(2)}) async-start(), calls=%async_computation.1 | async-start | bytes 14155776 | tf_op jit(solution)/shard_map/psum | solution.py:110
  136.8 15.8 %copy-start.7 = (f32[1536,768]{0,1:T(8,128)S(1)}, f32[1536,768]{0,1:T(8,128)}, u32[]{:S(2)}) copy-start(f32[1536,768]{0,1:T(8,128)} %all-reduce.4.cloned.1.call-done) | copy-start | bytes 14155780
  399.8 49.1 %copy-start.6 = (f32[384,384]{1,0:T(8,128)S(1)}, f32[384,384]{1,0:T(8,128)}, u32[]{:S(2)}) copy-start(f32[384,384]{1,0:T(8,128)} %get-tuple-element.6) | copy-start | bytes 1769476
  400.1 59.8 %slice-start.1 = ((s8[4718592]{0:T(1024)(128)(4,1)}), s8[524288]{0:T(1024)(128)(4,1)S(1)}, s32[]{:S(2)}) async-start(s8[4718592]{0:T(1024)(128)(4,1)} %bitcast.40), calls=%async_computation.3 | async-start | bytes 1048576
  448.9 11.1 %slice-start.2 = ((s8[4718592]{0:T(1024)(128)(4,1)}), s8[4194304]{0:T(1024)(128)(4,1)S(1)}, s32[]{:S(2)}) async-start(s8[4718592]{0:T(1024)(128)(4,1)} %bitcast.40), calls=%async_computation.4 | async-start | bytes 8388608
  454.6 5.3 copy-start.3
  467.5 6.5 %copy-start.8 = (f32[384,384]{1,0:T(8,128)S(1)}, f32[384,384]{1,0:T(8,128)}, u32[]{:S(2)}) copy-start(f32[384,384]{1,0:T(8,128)} %get-tuple-element.7) | copy-start | bytes 1769476
  482.5 7.8 %copy-start.4 = (f32[384,4,384]{2,0,1:T(8,128)S(1)}, f32[384,4,384]{2,0,1:T(8,128)}, u32[]{:S(2)}) copy-start(f32[384,4,384]{2,0,1:T(8,128)} %copy-done.3) | copy-start | bytes 7077892
  482.5 7.8 %copy-start.9 = (f32[384,384]{1,0:T(8,128)S(1)}, f32[384,384]{1,0:T(8,128)}, u32[]{:S(2)}) copy-start(f32[384,384]{1,0:T(8,128)} %get-tuple-element.8) | copy-start | bytes 1769476
  490.3 2.8 copy-start
  490.3 4.1 copy-start.1
  514.2 17.6 %copy-start.2 = (f32[384,4,384]{2,0,1:T(8,128)S(1)}, f32[384,4,384]{2,0,1:T(8,128)}, u32[]{:S(2)}) copy-start(f32[384,4,384]{2,0,1:T(8,128)} %fusion.13) | copy-start | bytes 7077892
  514.2 17.6 %copy-start.10 = (f32[384,384]{1,0:T(8,128)S(1)}, f32[384,384]{1,0:T(8,128)}, u32[]{:S(2)}) copy-start(f32[384,384]{1,0:T(8,128)} %get-tuple-element.9) | copy-start | bytes 1769476
  531.7 1.7 copy-start.5
Sparse Core Ops, SparseCore 0:
  18.9 117.8 all-reduce.3
  167.8 174.6 all-reduce.5

commit v5 on v4

--- a/solution.py
+++ b/solution.py
@@ -99,35 +99,33 @@
     glob = jnp.arange(count, dtype=jnp.int32) * ncol + column
     own = matrix[:, 0, :]
     zero = jnp.zeros_like(own)
-    both = lax.psum(
-        jnp.concatenate(
-            [jnp.where(column == 0, own, zero), jnp.where(column == 1, own, zero)], axis=1
-        ),
-        "col",
+    panel0, panel1 = lax.psum(
+        (jnp.where(column == 0, own, zero), jnp.where(column == 1, own, zero)), "col"
     )
-    gram_part = jnp.dot(both.T, both, precision=highest, preferred_element_type=jnp.float32)
-    cross_part = jnp.einsum("mb,mjt->bjt", both, matrix, precision=lax.Precision.HIGH)
-    gram, cross = lax.psum((gram_part, cross_part), "row")
-    g00 = gram[:width, :width]
-    g10 = gram[width:, :width]
-    g11 = gram[width:, width:]
+    high = lax.Precision.HIGH
+    parts = (
+        jnp.dot(panel0.T, panel0, precision=highest, preferred_element_type=jnp.float32),
+        jnp.dot(panel1.T, panel0, precision=highest, preferred_element_type=jnp.float32),
+        jnp.dot(panel1.T, panel1, precision=highest, preferred_element_type=jnp.float32),
+        jnp.einsum("mb,mjt->bjt", panel0, matrix, precision=high),
+        jnp.einsum("mb,mjt->bjt", panel1, matrix, precision=high),
+    )
+    g00, g10, g11, cross0, cross1 = lax.psum(parts, "row")
     upper0, inv0 = chol_inv(symmetric(g00))
     xmat = jnp.dot(g10, inv0.T, precision=highest, preferred_element_type=jnp.float32)
     schur = g11 - jnp.dot(xmat, xmat.T, precision=highest, preferred_element_type=jnp.float32)
     upper1, inv1 = chol_inv(symmetric(schur))
-    proj0 = jnp.einsum("ab,bjt->ajt", inv0, cross[:width], precision=highest)
-    rest1 = cross[width:] - jnp.einsum("ab,bjt->ajt", xmat, proj0, precision=highest)
-    proj1 = jnp.einsum("ab,bjt->ajt", inv1, rest1, precision=highest)
-    panel0 = both[:, :width]
-    panel1 = both[:, width:]
-    basis0 = jnp.dot(panel0, inv0.T, precision=highest, preferred_element_type=jnp.float32)
-    resid1 = panel1 - jnp.dot(basis0, xmat.T, precision=highest, preferred_element_type=jnp.float32)
-    basis1 = jnp.dot(resid1, inv1.T, precision=highest, preferred_element_type=jnp.float32)
+    proj0 = jnp.einsum("ab,bjt->ajt", inv0, cross0, precision=high)
+    rest1 = cross1 - jnp.einsum("ab,bjt->ajt", xmat, proj0, precision=high)
+    proj1 = jnp.einsum("ab,bjt->ajt", inv1, rest1, precision=high)
+    basis0 = jnp.dot(panel0, inv0.T, precision=high, preferred_element_type=jnp.float32)
+    resid1 = panel1 - jnp.dot(basis0, xmat.T, precision=high, preferred_element_type=jnp.float32)
+    basis1 = jnp.dot(resid1, inv1.T, precision=high, preferred_element_type=jnp.float32)
     kept0 = jnp.where((glob > 0)[None, :, None], proj0, jnp.float32(0.0))
     kept1 = jnp.where((glob > 1)[None, :, None], proj1, jnp.float32(0.0))
     basis = jnp.concatenate([basis0, basis1], axis=1)
     kept = jnp.concatenate([kept0, kept1], axis=0)
-    blocks = matrix - jnp.einsum("mb,bjt->mjt", basis, kept, precision=lax.Precision.HIGH)
+    blocks = matrix - jnp.einsum("mb,bjt->mjt", basis, kept, precision=high)
     blocks = jnp.where((glob == 0)[None, :, None], basis0[:, None, :], blocks)
     blocks = jnp.where((glob == 1)[None, :, None], basis1[:, None, :], blocks)
     row0 = jnp.where((glob == 0)[None, :, None], upper0[:, None, :], kept0)

time: 553 us -> 548 us (level)
    unnamed x29 -> x39, local copies, waits for them, and re-layouts: 30.6 us -> 33.6 us
    dot_general x9 -> x12, matrix products: 86.7 us -> 85.4 us  [the longest x1 19.8 us: shards(): blocks = matrix - jnp.einsum('mb,bjt->mjt', basis, kept, precision=high)]
where the time goes in v5:
time: 548 us; the launch traced here: 539 us
  waiting for transfers between devices  288 us (53%)
  Pallas kernels  95.7 us (17%)
  matrix products  87.9 us (16%)
  local copies, waits for them, and re-layouts  41.1 us (8%)
  between operations  14.6 us (3%)
  other arithmetic  11.4 us (2%)
    psum x1, waiting for transfers between devices, shards(): g00, g10, g11, cross0, cross1 = lax.psum(parts, 'row')  170 us
    psum x1, waiting for transfers between devices, shards(): lax.psum((jnp.where(column == 0, own, zero), jnp.where(column == 1, own,...  118 us
    pallas_call x2, Pallas kernels, chol_inv(): pl.pallas_call(_chol_inv_kernel, out_shape=(jax.ShapeDtypeStruct((n, n),...  95.7 us
    unnamed x39, local copies, waits for them, and re-layouts  33.6 us
    dot_general x1, matrix products, shards(): blocks = matrix - jnp.einsum('mb,bjt->mjt', basis, kept, precision=high)  19.8 us
  transfers between devices with their start and end apart: 2, of which 2 were waited for; matrix products, arithmetic and copies ran while one was open for 0% of the time, Pallas kernels for 0%

profile of v5, /device:TPU:0, one launch (start us, length us, event | category | flops | bytes accessed | tf_op | source)
XLA Modules:
  0.0 538.5 jit_solution(5687962195665827549)
XLA Ops:
  7.2 8.0 %copy.14 = f32[1536,4,384]{2,0,1:T(8,128)} copy(f32[1536,4,384]{2,1,0:T(4,128)} %param.1) | data formatting | bytes 18874368 | tf_op args[0]
  15.2 4.2 select_bitcast_fusion.2
  19.5 118.0 %all-reduce.7.cloned.1.call-done = (f32[1536,384]{1,0:T(8,128)}, f32[1536,384]{1,0:T(8,128)}) async-done(((f32[1536,384]{1,0:T(8,128)}, f32[1536,384]{1,0:T(8,128)}), (f32[1536,384]{1,0:T(8,128)}, f32[1536,384]{1,0:T(8,128)})) %all-reduce.7.cloned.1.call-update) | async-done | bytes 4718608 | tf_op jit(solution)/shard_map/psum | solution.py:102
  137.6 7.3 %fusion.24 = f32[384,384]{0,1:T(8,128)} fusion(f32[1536,384]{1,0:T(8,128)} %get-tuple-element.20), kind=kOutput, calls=%fused_computation.39 | convolution fusion | flops 2717908992 | bytes 2949120 | tf_op jit(solution)/shard_map/dot_general | solution.py:107
  144.8 7.2 %fusion.26 = f32[384,384]{1,0:T(8,128)} fusion(f32[1536,384]{1,0:T(8,128)} %get-tuple-element.19, f32[1536,384]{1,0:T(8,128)} %get-tuple-element.20), kind=kOutput, calls=%fused_computation.41 | convolution fusion | flops 2717908992 | bytes 5308416 | tf_op jit(solution)/shard_map/dot_general | solution.py:108
  152.1 5.2 fusion.28
  157.3 8.2 %fusion.5 = f32[384,4,384]{2,0,1:T(8,128)} fusion(f32[1536,384]{1,0:T(8,128)S(1)} %copy-done.2, f32[1536,4,384]{2,1,0:T(4,128)S(1)} %bitcast.53), kind=kOutput, calls=%fused_computation.9 | convolution fusion | flops 5435817984 | bytes 14155776 | tf_op jit(solution)/shard_map/mb,mjt->bjt/dot_general | solution.py:111
  165.5 8.3 %fusion.7 = f32[384,4,384]{2,0,1:T(8,128)} fusion(f32[1536,384]{1,0:T(8,128)S(1)} %copy-done.3, f32[1536,4,384]{2,1,0:T(4,128)S(1)} %bitcast.53), kind=kOutput, calls=%fused_computation.11 | convolution fusion | flops 5435817984 | bytes 14155776 | tf_op jit(solution)/shard_map/mb,mjt->bjt/dot_general | solution.py:110
  173.9 169.7 %all-reduce.5.cloned.1.call-done = (f32[384,384]{0,1:T(8,128)}, f32[384,384]{1,0:T(8,128)}, f32[384,384]{0,1:T(8,128)}, f32[384,4,384]{2,0,1:T(8,128)}, f32[384,4,384]{2,0,1:T(8,128)}) async-done(((f32[384,384]{0,1:T(8,128)}, f32[384,384]{1,0:T(8,128)}, f32[384,384]{0,1:T(8,128)}, f32[384,4,384]{2,0,1:T(8,128)}, f32[384,4,384]{2,0,1:T(8,128)}), (f32[384,384]{0,1:T(8,128)}, f32[384,384]{1,0:T(8,128)}, ...) | async-done | bytes 6488080 | tf_op jit(solution)/shard_map/psum | solution.py:113
  343.6 1.3 copy.16
  344.9 1.9 fusion.20.a_ref
  346.8 47.8 %shard_map.30 = (f32[384,384]{1,0:T(8,128)}, f32[384,384]{1,0:T(8,128)}) custom-call(f32[384,384]{1,0:T(8,128)} %fusion.20.a_ref), custom_call_target="tpu_custom_call" | custom-call | flops 113246208 | bytes 1769472 | tf_op jit(solution)/shard_map/pallas_call | solution.py:76
  394.6 4.6 fusion.25
  399.2 1.3 fusion.27
  400.5 2.0 copy.21
  402.5 7.7 %convolution_subtract_fusion = f32[1536,384]{1,0:T(8,128)} fusion(f32[1536,384]{1,0:T(8,128)} %get-tuple-element.19, f32[1536,384]{0,1:T(8,128)} %fusion.25, f32[384,384]{1,0:T(8,128)S(1)} %fusion.27), kind=kOutput, calls=%fused_computation.8 | convolution fusion | flops 1359544320 | bytes 7667712 | tf_op jit(solution)/shard_map/dot_general | solution.py:122
  410.3 1.3 convolution_subtract_fusion.1
  411.5 1.1 copy.19
  412.6 1.9 fusion.19.a_ref
  414.5 47.9 %shard_map.31 = (f32[384,384]{1,0:T(8,128)}, f32[384,384]{1,0:T(8,128)}) custom-call(f32[384,384]{1,0:T(8,128)} %fusion.19.a_ref), custom_call_target="tpu_custom_call" | custom-call | flops 113246208 | bytes 1769472 | tf_op jit(solution)/shard_map/pallas_call | solution.py:76
  462.5 4.0 fusion.17
  466.5 3.6 fusion.14
  470.1 3.4 fusion.29
  473.6 3.1 copy.20
  476.7 6.0 %fusion.11 = f32[384,4,384]{2,0,1:T(8,128)} fusion(f32[384,4,384]{2,0,1:T(8,128)} %get-tuple-element.17, f32[384,4,384]{2,0,1:T(8,128)} %fusion.14, pred[4]{0:T(512)(128)(4,1)S(1)} %get-tuple-element.26, f32[384,384]{1,0:T(8,128)S(1)} %copy-done.10), kind=kOutput, calls=%fused_computation.19 | convolution fusion | flops 1360134144 | bytes 7667716 | tf_op jit(solution)/shard_map/ab,bjt->ajt/dot_general | solution.py:120
  482.7 2.8 select_bitcast_fusion.1
  485.4 1.3 copy-done.1
  486.7 19.8 %select_select_fusion = f32[1536,4,384]{2,0,1:T(8,128)} fusion(f32[1536,384]{0,1:T(8,128)} %fusion.29, f32[1536,384]{0,1:T(8,128)S(1)} %copy-done.1, f32[384,4,384]{2,0,1:T(8,128)} %fusion.11, f32[384,4,384]{2,0,1:T(8,128)} %get-tuple-element.22, f32[1536,384]{1,0:T(8,128)S(1)} %copy.21, f32[1536,384]{1,0:T(8,128)S(1)} %copy-done, ...), kind=kOutput, calls=%fused_computation | convolution fusion | flops 10881073152 | bytes 33030152 | tf_op jit(solution)/shard_map/mb,bjt->mjt/dot_general | solution.py:128
  506.5 17.5 %copy.24 = f32[1536,4,384]{2,1,0:T(4,128)} copy(f32[1536,4,384]{2,0,1:T(8,128)} %select_select_fusion) | data formatting | bytes 18874368
  524.3 1.4 copy-done.7
  525.7 0.3 pad_maximum_fusion
  526.0 5.2 copy.25
  (43 shorter events, 0.4 us)
Async XLA Ops:
  7.2 130.4 %all-reduce.7.cloned.1.call-start = ((), (), s32[]{:S(2)}) async-start(), calls=%async_computation.1 | async-start | bytes 9437184 | tf_op jit(solution)/shard_map/psum | solution.py:102
  19.4 137.8 %slice-start = ((s8[9437184]{0:T(1024)(128)(4,1)}), s8[1048576]{0:T(1024)(128)(4,1)S(1)}, s32[]{:S(2)}) async-start(s8[9437184]{0:T(1024)(128)(4,1)} %bitcast.52), calls=%async_computation.2 | async-start | bytes 2097152
  19.5 324.1 %all-reduce.5.cloned.1.call-start = ((), (), s32[]{:S(2)}) async-start(), calls=%async_computation | async-start | bytes 12976128 | tf_op jit(solution)/shard_map/psum | solution.py:113
  137.6 14.5 %copy-start.2 = (f32[1536,384]{1,0:T(8,128)S(1)}, f32[1536,384]{1,0:T(8,128)}, u32[]{:S(2)}) copy-start(f32[1536,384]{1,0:T(8,128)} %get-tuple-element.19) | copy-start | bytes 7077892
  137.6 19.7 %slice-start.1 = ((s8[9437184]{0:T(1024)(128)(4,1)}), s8[4194304]{0:T(1024)(128)(4,1)S(1)}, s32[]{:S(2)}) async-start(s8[9437184]{0:T(1024)(128)(4,1)} %bitcast.52), calls=%async_computation.3 | async-start | bytes 8388608
  144.8 12.4 %slice-start.2 = ((s8[9437184]{0:T(1024)(128)(4,1)}), s8[4194304]{0:T(1024)(128)(4,1)S(1)}, s32[]{:S(2)}) async-start(s8[9437184]{0:T(1024)(128)(4,1)} %bitcast.52), calls=%async_computation.4 | async-start | bytes 8388608
  157.3 8.2 %copy-start.3 = (f32[1536,384]{1,0:T(8,128)S(1)}, f32[1536,384]{1,0:T(8,128)}, u32[]{:S(2)}) copy-start(f32[1536,384]{1,0:T(8,128)} %get-tuple-element.20) | copy-start | bytes 7077892
  394.6 4.6 copy-start.9
  394.6 4.6 copy-start.12
  402.5 7.8 %copy-start.13 = (f32[384,384]{0,1:T(8,128)S(1)}, f32[384,384]{0,1:T(8,128)}, u32[]{:S(2)}) copy-start(f32[384,384]{0,1:T(8,128)} %get-tuple-element.16) | copy-start | bytes 1769476
  466.4 3.7 copy-start.5
  466.4 3.7 copy-start.8
  466.4 3.7 copy-start.10
  476.6 6.0 %copy-start.6 = (f32[384,4,384]{2,0,1:T(8,128)S(1)}, f32[384,4,384]{2,0,1:T(8,128)}, u32[]{:S(2)}) copy-start(f32[384,4,384]{2,0,1:T(8,128)} %copy-done.5) | copy-start | bytes 7077892
  476.7 6.0 %copy-start.11 = (f32[384,384]{1,0:T(8,128)S(1)}, f32[384,384]{1,0:T(8,128)}, u32[]{:S(2)}) copy-start(f32[384,384]{1,0:T(8,128)} %get-tuple-element.8) | copy-start | bytes 1769476
  482.6 2.8 copy-start
  482.6 4.1 copy-start.1
  506.5 17.6 %copy-start.4 = (f32[384,4,384]{2,0,1:T(8,128)S(1)}, f32[384,4,384]{2,0,1:T(8,128)}, u32[]{:S(2)}) copy-start(f32[384,4,384]{2,0,1:T(8,128)} %fusion.11) | copy-start | bytes 7077892
  506.5 17.6 %copy-start.14 = (f32[384,384]{1,0:T(8,128)S(1)}, f32[384,384]{1,0:T(8,128)}, u32[]{:S(2)}) copy-start(f32[384,384]{1,0:T(8,128)} %get-tuple-element.9) | copy-start | bytes 1769476
  524.1 1.7 copy-start.7
Sparse Core Ops, SparseCore 0:
  19.6 117.9 all-reduce.6
  174.0 169.5 all-reduce.4

commit v6 on v5

--- a/solution.py
+++ b/solution.py
@@ -2,6 +2,7 @@
 import jax.numpy as jnp
 from jax import lax
 from jax.sharding import PartitionSpec as P
+from jax.experimental.layout import Layout, with_layout_constraint
 from jax.experimental import pallas as pl
 from jax.experimental.pallas import tpu as pltpu
 
@@ -128,9 +129,11 @@
     blocks = matrix - jnp.einsum("mb,bjt->mjt", basis, kept, precision=high)
     blocks = jnp.where((glob == 0)[None, :, None], basis0[:, None, :], blocks)
     blocks = jnp.where((glob == 1)[None, :, None], basis1[:, None, :], blocks)
+    blocks = with_layout_constraint(blocks, Layout(major_to_minor=(0, 1, 2)))
     row0 = jnp.where((glob == 0)[None, :, None], upper0[:, None, :], kept0)
     row1 = jnp.where((glob == 1)[None, :, None], upper1[:, None, :], kept1)
-    return (blocks, jnp.stack([row0, row1]))
+    rows = with_layout_constraint(jnp.stack([row0, row1]), Layout(major_to_minor=(0, 1, 2, 3)))
+    return (blocks, rows)
 
 
 def solution(mesh):

time: 548 us -> 547 us (level)
  other arithmetic: 11.4 us -> 43.3 us
  local copies, waits for them, and re-layouts: 41.1 us -> 13.5 us
    unnamed x39 -> x49, local copies, waits for them, and re-layouts: 33.6 us -> 4.39 us
    select_n x0 -> x1, other arithmetic: none -> 24.5 us  [shards(): blocks = jnp.where((glob == 1)[None, :, None], basis1[:, None, :], blocks)]
    another operation x3, other arithmetic: 3.32 us -> 8.97 us  [shards(): jnp.stack([row0, row1])]
where the time goes in v6:
time: 547 us; the launch traced here: 538 us
  waiting for transfers between devices  288 us (53%)
  Pallas kernels  95.5 us (17%)
  matrix products  82.6 us (15%)
  other arithmetic  43.3 us (8%)
  between operations  14.7 us (3%)
  local copies, waits for them, and re-layouts  13.5 us (2%)
    psum x1, waiting for transfers between devices, shards(): g00, g10, g11, cross0, cross1 = lax.psum(parts, 'row')  170 us
    psum x1, waiting for transfers between devices, shards(): lax.psum((jnp.where(column == 0, own, zero), jnp.where(column == 1, own,...  118 us
    pallas_call x2, Pallas kernels, chol_inv(): pl.pallas_call(_chol_inv_kernel, out_shape=(jax.ShapeDtypeStruct((n, n),...  95.5 us
    select_n x1, other arithmetic, shards(): blocks = jnp.where((glob == 1)[None, :, None], basis1[:, None, :], blocks)  24.5 us
    dot_general x1, matrix products, shards(): blocks = matrix - jnp.einsum('mb,bjt->mjt', basis, kept, precision=high)  15.1 us
  transfers between devices with their start and end apart: 2, of which 2 were waited for; matrix products, arithmetic and copies ran while one was open for 0% of the time, Pallas kernels for 0%

profile of v6, /device:TPU:0, one launch (start us, length us, event | category | flops | bytes accessed | tf_op | source)
XLA Modules:
  0.0 537.7 jit_solution(8689531025457489414)
XLA Ops:
  7.2 4.3 copy.15
  11.5 2.5 select_bitcast_fusion.2
  14.0 0.0 all-reduce.5.cloned.1.call-start
  14.1 118.0 %all-reduce.7.cloned.1.call-done = (f32[1536,384]{1,0:T(8,128)}, f32[1536,384]{1,0:T(8,128)}) async-done(((f32[1536,384]{1,0:T(8,128)}, f32[1536,384]{1,0:T(8,128)}), (f32[1536,384]{1,0:T(8,128)}, f32[1536,384]{1,0:T(8,128)})) %all-reduce.7.cloned.1.call-update) | async-done | bytes 4718608 | tf_op jit(solution)/shard_map/psum | solution.py:103
  132.1 7.2 %fusion.26 = f32[384,384]{0,1:T(8,128)} fusion(f32[1536,384]{1,0:T(8,128)} %get-tuple-element.15), kind=kOutput, calls=%fused_computation.45 | convolution fusion | flops 2717908992 | bytes 2949120 | tf_op jit(solution)/shard_map/dot_general | solution.py:110
  139.3 7.2 %fusion.24 = f32[384,384]{1,0:T(8,128)} fusion(f32[1536,384]{1,0:T(8,128)} %get-tuple-element.15, f32[1536,384]{1,0:T(8,128)} %get-tuple-element.16), kind=kOutput, calls=%fused_computation.43 | convolution fusion | flops 2717908992 | bytes 5308416 | tf_op jit(solution)/shard_map/dot_general | solution.py:109
  146.6 5.1 fusion.22
  151.7 8.1 %fusion.6 = f32[384,4,384]{2,0,1:T(8,128)} fusion(f32[1536,384]{1,0:T(8,128)S(1)} %copy-done, f32[1536,4,384]{2,1,0:T(4,128)S(1)} %bitcast.53), kind=kOutput, calls=%fused_computation.11 | convolution fusion | flops 5435817984 | bytes 14155776 | tf_op jit(solution)/shard_map/mb,mjt->bjt/dot_general | solution.py:112
  159.8 8.5 %fusion.8 = f32[384,4,384]{2,0,1:T(8,128)} fusion(f32[1536,384]{1,0:T(8,128)S(1)} %copy-done.1, f32[1536,4,384]{2,1,0:T(4,128)S(1)} %bitcast.53), kind=kOutput, calls=%fused_computation.13 | convolution fusion | flops 5435817984 | bytes 14155776 | tf_op jit(solution)/shard_map/mb,mjt->bjt/dot_general | solution.py:111
  168.3 169.9 %all-reduce.5.cloned.1.call-done = (f32[384,384]{0,1:T(8,128)}, f32[384,384]{1,0:T(8,128)}, f32[384,384]{0,1:T(8,128)}, f32[384,4,384]{2,0,1:T(8,128)}, f32[384,4,384]{2,0,1:T(8,128)}) async-done(((f32[384,384]{0,1:T(8,128)}, f32[384,384]{1,0:T(8,128)}, f32[384,384]{0,1:T(8,128)}, f32[384,4,384]{2,0,1:T(8,128)}, f32[384,4,384]{2,0,1:T(8,128)}), (f32[384,384]{0,1:T(8,128)}, f32[384,384]{1,0:T(8,128)}, ...) | async-done | bytes 6488080 | tf_op jit(solution)/shard_map/psum | solution.py:114
  338.3 1.3 copy.17
  339.6 1.9 fusion.18.a_ref
  341.5 47.8 %shard_map.30 = (f32[384,384]{1,0:T(8,128)}, f32[384,384]{1,0:T(8,128)}) custom-call(f32[384,384]{1,0:T(8,128)} %fusion.18.a_ref), custom_call_target="tpu_custom_call" | custom-call | flops 113246208 | bytes 1769472 | tf_op jit(solution)/shard_map/pallas_call | solution.py:77
  389.3 5.4 fusion.23
  394.6 1.3 fusion.25
  395.9 3.6 fusion.15
  399.5 3.4 copy.22
  403.0 7.0 %convolution_subtract_fusion = f32[1536,384]{1,0:T(8,128)} fusion(f32[1536,384]{1,0:T(8,128)S(1)} %copy-done, f32[1536,384]{0,1:T(8,128)} %fusion.23, f32[384,384]{1,0:T(8,128)S(1)} %fusion.25), kind=kOutput, calls=%fused_computation.10 | convolution fusion | flops 1359544320 | bytes 7667712 | tf_op jit(solution)/shard_map/dot_general | solution.py:123
  410.0 2.7 convolution_subtract_fusion.1
  412.7 1.1 copy.20
  413.8 2.0 fusion.17.a_ref
  415.8 47.8 %shard_map.31 = (f32[384,384]{1,0:T(8,128)}, f32[384,384]{1,0:T(8,128)}) custom-call(f32[384,384]{1,0:T(8,128)} %fusion.17.a_ref), custom_call_target="tpu_custom_call" | custom-call | flops 113246208 | bytes 1769472 | tf_op jit(solution)/shard_map/pallas_call | solution.py:77
  463.6 3.4 fusion.12
  467.0 3.5 fusion.27
  470.5 3.2 copy.21
  473.8 4.5 fusion.10
  478.3 3.6 select_bitcast_fusion.1
  481.9 2.1 select_bitcast_fusion
  484.1 3.4 pad_maximum_fusion
  487.5 15.1 %fusion.2 = f32[1536,4,384]{2,0,1:T(8,128)S(1)} fusion(f32[1536,384]{0,1:T(8,128)S(1)} %copy-done.8, f32[1536,384]{0,1:T(8,128)S(1)} %copy-done.2, f32[768,4,384]{2,1,0:T(4,128)} %pad_maximum_fusion), kind=kOutput, calls=%fused_computation.4 | convolution fusion | flops 10872815616 | bytes 18874368 | tf_op jit(solution)/shard_map/mb,bjt->mjt/dot_general | solution.py:129
  502.6 3.3 pad_maximum_fusion.1
  505.9 24.5 %fusion.1 = f32[1536,4,384]{2,1,0:T(4,128)} fusion(f32[1536,4,384]{2,1,0:T(4,128)S(1)} %bitcast.55, f32[1536,4,384]{2,0,1:T(8,128)S(1)} %fusion.2, f32[1536,384]{1,0:T(8,128)S(1)} %copy-done.6, f32[1536,384]{1,0:T(8,128)S(1)} %copy-done.7, pred[4]{0:T(512)(128)(4,1)S(1)} %get-tuple-element.25, pred[4]{0:T(512)(128)(4,1)S(1)} %get-tuple-element.26), kind=kLoop, calls=%fused_computation.2 | loop fusion | flops 7077888 | bytes 33030152 | tf_op jit(solution)/shard_map/jit(_where)/select_n | solution.py:131
  (55 shorter events, 0.2 us)
Async XLA Ops:
  7.2 124.9 %all-reduce.7.cloned.1.call-start = ((), (), s32[]{:S(2)}) async-start(), calls=%async_computation.1 | async-start | bytes 9437184 | tf_op jit(solution)/shard_map/psum | solution.py:103
  14.0 137.7 %slice-start = ((s8[9437184]{0:T(1024)(128)(4,1)}), s8[1048576]{0:T(1024)(128)(4,1)S(1)}, s32[]{:S(2)}) async-start(s8[9437184]{0:T(1024)(128)(4,1)} %bitcast.52), calls=%async_computation.2 | async-start | bytes 2097152
  14.0 324.2 %all-reduce.5.cloned.1.call-start = ((), (), s32[]{:S(2)}) async-start(), calls=%async_computation | async-start | bytes 12976128 | tf_op jit(solution)/shard_map/psum | solution.py:114
  132.1 14.5 %copy-start.1 = (f32[1536,384]{1,0:T(8,128)S(1)}, f32[1536,384]{1,0:T(8,128)}, u32[]{:S(2)}) copy-start(f32[1536,384]{1,0:T(8,128)} %get-tuple-element.16) | copy-start | bytes 7077892
  132.1 19.5 %slice-start.1 = ((s8[9437184]{0:T(1024)(128)(4,1)}), s8[4194304]{0:T(1024)(128)(4,1)S(1)}, s32[]{:S(2)}) async-start(s8[9437184]{0:T(1024)(128)(4,1)} %bitcast.52), calls=%async_computation.3 | async-start | bytes 8388608
  139.3 12.3 %slice-start.2 = ((s8[9437184]{0:T(1024)(128)(4,1)}), s8[4194304]{0:T(1024)(128)(4,1)S(1)}, s32[]{:S(2)}) async-start(s8[9437184]{0:T(1024)(128)(4,1)} %bitcast.52), calls=%async_computation.4 | async-start | bytes 8388608
  146.6 5.1 copy-start
  389.3 5.4 copy-start.11
  389.3 5.4 copy-start.16
  389.3 6.6 %copy-start.12 = (f32[384,4,384]{2,0,1:T(8,128)S(1)}, f32[384,4,384]{2,0,1:T(8,128)}, u32[]{:S(2)}) copy-start(f32[384,4,384]{2,0,1:T(8,128)} %get-tuple-element.14) | copy-start | bytes 7077892
  395.9 14.1 %copy-start.4 = (f32[384,384]{1,0:T(8,128)}, f32[384,384]{1,0:T(8,128)S(1)}, u32[]{:S(2)}) copy-start(f32[384,384]{1,0:T(8,128)S(1)} %fusion.25) | copy-start | bytes 1769476
  403.0 7.0 %copy-start.17 = (f32[384,384]{0,1:T(8,128)S(1)}, f32[384,384]{0,1:T(8,128)}, u32[]{:S(2)}) copy-start(f32[384,384]{0,1:T(8,128)} %get-tuple-element.12) | copy-start | bytes 1769476
  410.0 53.6 %copy-start.3 = (f32[384,4,384]{2,0,1:T(8,128)S(1)}, f32[384,4,384]{2,0,1:T(8,128)}, u32[]{:S(2)}) copy-start(f32[384,4,384]{2,0,1:T(8,128)} %fusion.15) | copy-start | bytes 7077892
  410.0 53.6 %copy-start.5 = (f32[384,384]{1,0:T(8,128)S(1)}, f32[384,384]{1,0:T(8,128)}, u32[]{:S(2)}) copy-start(f32[384,384]{1,0:T(8,128)} %copy-done.4) | copy-start | bytes 1769476
  463.6 3.5 copy-start.10
  463.6 3.5 copy-start.13
  473.8 4.5 copy-start.14
  478.3 3.6 copy-start.15
  484.0 3.4 copy-start.2
  484.0 3.4 copy-start.8
  484.1 21.8 %slice-start.3 = ((s8[9437184]{0:T(1024)(128)(4,1)}), s8[1048576]{0:T(1024)(128)(4,1)S(1)}, s32[]{:S(2)}) async-start(s8[9437184]{0:T(1024)(128)(4,1)} %bitcast.54), calls=%async_computation.5 | async-start | bytes 2097152
  487.5 15.1 %copy-start.9 = (f32[1,384,4,384]{3,2,1,0:T(4,128)S(1)}, f32[1,384,4,384]{3,2,1,0:T(4,128)}, u32[]{:S(2)}) copy-start(f32[1,384,4,384]{3,2,1,0:T(4,128)} %get-tuple-element.17) | copy-start | bytes 7077892
  487.5 18.4 %slice-start.4 = ((s8[9437184]{0:T(1024)(128)(4,1)}), s8[4194304]{0:T(1024)(128)(4,1)S(1)}, s32[]{:S(2)}) async-start(s8[9437184]{0:T(1024)(128)(4,1)} %bitcast.54), calls=%async_computation.6 | async-start | bytes 8388608
  487.5 18.4 %slice-start.5 = ((s8[9437184]{0:T(1024)(128)(4,1)}), s8[4194304]{0:T(1024)(128)(4,1)S(1)}, s32[]{:S(2)}) async-start(s8[9437184]{0:T(1024)(128)(4,1)} %bitcast.54), calls=%async_computation.7 | async-start | bytes 8388608
  502.6 3.3 copy-start.6
  502.6 3.3 copy-start.7
Sparse Core Ops, SparseCore 0:
  14.1 117.9 all-reduce.6
  168.4 169.8 all-reduce.4

commit v7 on v6

--- a/solution.py
+++ b/solution.py
@@ -16,10 +16,10 @@
     return jnp.dot(a, b, precision=lax.Precision.HIGHEST, preferred_element_type=jnp.float32)
 
 
-def _chol_inv_kernel(a_ref, u_ref, m_ref, w_ref, t_ref, d_ref, e_ref):
-    n = a_ref.shape[0]
+def _factor(a, u_ref, m_ref, w_ref, t_ref, d_ref, e_ref):
+    n = a.shape[0]
     nb = n // TILE
-    w_ref[...] = a_ref[...]
+    w_ref[...] = a
     u_ref[...] = jnp.zeros_like(u_ref)
     m_ref[...] = jnp.zeros_like(m_ref)
     rows = lax.broadcasted_iota(jnp.int32, (TILE, TILE), 0)
@@ -72,23 +72,29 @@
             m_ref[i * TILE:(i + 1) * TILE, j * TILE:(j + 1) * TILE] = -_mm(di, acc)
 
 
-def chol_inv(a):
-    n = a.shape[0]
+def _pair_kernel(g00_ref, g10_ref, g11_ref, u0_ref, m0_ref, x_ref, u1_ref, m1_ref, w_ref, t_ref, d_ref, e_ref):
+    g00 = g00_ref[...]
+    _factor((g00 + g00.T) * 0.5, u0_ref, m0_ref, w_ref, t_ref, d_ref, e_ref)
+    xmat = _mm(g10_ref[...], m0_ref[...].T)
+    x_ref[...] = xmat
+    schur = g11_ref[...] - _mm(xmat, xmat.T)
+    _factor((schur + schur.T) * 0.5, u1_ref, m1_ref, w_ref, t_ref, d_ref, e_ref)
+
+
+def factor_pair(g00, g10, g11):
+    n = g00.shape[0]
+    square = jax.ShapeDtypeStruct((n, n), jnp.float32)
     return pl.pallas_call(
-        _chol_inv_kernel,
-        out_shape=(jax.ShapeDtypeStruct((n, n), jnp.float32), jax.ShapeDtypeStruct((n, n), jnp.float32)),
+        _pair_kernel,
+        out_shape=(square,) * 5,
         scratch_shapes=[
             pltpu.VMEM((n, n), jnp.float32),
             pltpu.VMEM((TILE, TILE), jnp.float32),
             pltpu.VMEM((TILE, TILE), jnp.float32),
             pltpu.VMEM((TILE, TILE), jnp.float32),
         ],
-        cost_estimate=pl.CostEstimate(flops=2 * n * n * n, bytes_accessed=3 * n * n * 4, transcendentals=n),
-    )(a)
-
-
-def symmetric(a):
-    return (a + a.T) * jnp.float32(0.5)
+        cost_estimate=pl.CostEstimate(flops=8 * n * n * n, bytes_accessed=8 * n * n * 4, transcendentals=2 * n),
+    )(g00, g10, g11)
 
 
 def shards(matrix):
@@ -112,10 +118,7 @@
         jnp.einsum("mb,mjt->bjt", panel1, matrix, precision=high),
     )
     g00, g10, g11, cross0, cross1 = lax.psum(parts, "row")
-    upper0, inv0 = chol_inv(symmetric(g00))
-    xmat = jnp.dot(g10, inv0.T, precision=highest, preferred_element_type=jnp.float32)
-    schur = g11 - jnp.dot(xmat, xmat.T, precision=highest, preferred_element_type=jnp.float32)
-    upper1, inv1 = chol_inv(symmetric(schur))
+    upper0, inv0, xmat, upper1, inv1 = factor_pair(g00, g10, g11)
     proj0 = jnp.einsum("ab,bjt->ajt", inv0, cross0, precision=high)
     rest1 = cross1 - jnp.einsum("ab,bjt->ajt", xmat, proj0, precision=high)
     proj1 = jnp.einsum("ab,bjt->ajt", inv1, rest1, precision=high)

time: 547 us -> 533 us (0.974)
  matrix products: 82.6 us -> 73.7 us
    pallas_call x2 -> x1, Pallas kernels: 95.5 us -> 96.7 us  [factor_pair(): pl.pallas_call(_pair_kernel, out_shape=(square,) * 5, scratch_shapes=[plt...]
where the time goes in v7:
time: 533 us; the launch traced here: 523 us
  waiting for transfers between devices  288 us (54%)
  Pallas kernels  96.7 us (18%)
  matrix products  73.7 us (14%)
  other arithmetic  39.4 us (7%)
  between operations  14.5 us (3%)
  local copies, waits for them, and re-layouts  11.1 us (2%)
    psum x1, waiting for transfers between devices, shards(): g00, g10, g11, cross0, cross1 = lax.psum(parts, 'row')  170 us
    psum x1, waiting for transfers between devices, shards(): lax.psum((jnp.where(column == 0, own, zero), jnp.where(column == 1, own,...  118 us
    pallas_call x1, Pallas kernels, factor_pair(): pl.pallas_call(_pair_kernel, out_shape=(square,) * 5, scratch_shapes=[plt...  96.7 us
    select_n x1, other arithmetic, shards(): blocks = jnp.where((glob == 1)[None, :, None], basis1[:, None, :], blocks)  24.5 us
    dot_general x1, matrix products, shards(): blocks = matrix - jnp.einsum('mb,bjt->mjt', basis, kept, precision=high)  15 us
  transfers between devices with their start and end apart: 2, of which 2 were waited for; matrix products, arithmetic and copies ran while one was open for 0% of the time, Pallas kernels for 0%

profile of v7, /device:TPU:0, one launch (start us, length us, event | category | flops | bytes accessed | tf_op | source)
XLA Modules:
  0.0 523.5 jit_solution(17903559254764554313)
XLA Ops:
  7.2 0.0 all-reduce.7.cloned.1.call-start
  7.2 4.3 copy.10
  11.5 2.5 select_bitcast_fusion.2
  14.0 0.0 all-reduce.7.cloned.1.call-update
  14.0 0.0 all-reduce.5.cloned.1.call-start
  14.1 118.0 %all-reduce.7.cloned.1.call-done = (f32[1536,384]{1,0:T(8,128)}, f32[1536,384]{1,0:T(8,128)}) async-done(((f32[1536,384]{1,0:T(8,128)}, f32[1536,384]{1,0:T(8,128)}), (f32[1536,384]{1,0:T(8,128)}, f32[1536,384]{1,0:T(8,128)})) %all-reduce.7.cloned.1.call-update) | async-done | bytes 4718608 | tf_op jit(solution)/shard_map/psum | solution.py:109
  132.1 7.2 %fusion.22 = f32[384,384]{1,0:T(8,128)} fusion(f32[1536,384]{1,0:T(8,128)} %get-tuple-element.17), kind=kOutput, calls=%fused_computation.38 | convolution fusion | flops 2717908992 | bytes 2949120 | tf_op jit(solution)/shard_map/dot_general | solution.py:116
  139.4 7.2 %fusion.21 = f32[384,384]{1,0:T(8,128)} fusion(f32[1536,384]{1,0:T(8,128)} %get-tuple-element.17, f32[1536,384]{1,0:T(8,128)} %get-tuple-element.18), kind=kOutput, calls=%fused_computation.37 | convolution fusion | flops 2717908992 | bytes 5308416 | tf_op jit(solution)/shard_map/dot_general | solution.py:115
  146.6 5.2 fusion.20
  151.8 8.1 %fusion.6 = f32[384,4,384]{2,0,1:T(8,128)} fusion(f32[1536,384]{1,0:T(8,128)S(1)} %copy-done, f32[1536,4,384]{2,1,0:T(4,128)S(1)} %bitcast.41), kind=kOutput, calls=%fused_computation.11 | convolution fusion | flops 5435817984 | bytes 14155776 | tf_op jit(solution)/shard_map/mb,mjt->bjt/dot_general | solution.py:118
  160.0 8.4 %fusion.8 = f32[384,4,384]{2,0,1:T(8,128)} fusion(f32[1536,384]{1,0:T(8,128)S(1)} %copy-done.1, f32[1536,4,384]{2,1,0:T(4,128)S(1)} %bitcast.41), kind=kOutput, calls=%fused_computation.13 | convolution fusion | flops 5435817984 | bytes 14155776 | tf_op jit(solution)/shard_map/mb,mjt->bjt/dot_general | solution.py:117
  168.4 0.0 all-reduce.5.cloned.1.call-update
  168.4 169.8 %all-reduce.5.cloned.1.call-done = (f32[384,384]{1,0:T(8,128)}, f32[384,384]{1,0:T(8,128)}, f32[384,384]{1,0:T(8,128)}, f32[384,4,384]{2,0,1:T(8,128)}, f32[384,4,384]{2,0,1:T(8,128)}) async-done(((f32[384,384]{1,0:T(8,128)}, f32[384,384]{1,0:T(8,128)}, f32[384,384]{1,0:T(8,128)}, f32[384,4,384]{2,0,1:T(8,128)}, f32[384,4,384]{2,0,1:T(8,128)}), (f32[384,384]{1,0:T(8,128)}, f32[384,384]{1,0:T(8,128)}, ...) | async-done | bytes 6488080 | tf_op jit(solution)/shard_map/psum | solution.py:120
  338.3 96.7 %shard_map.30 = (f32[384,384]{1,0:T(8,128)}, f32[384,384]{1,0:T(8,128)}, f32[384,384]{1,0:T(8,128)}, f32[384,384]{1,0:T(8,128)}, f32[384,384]{1,0:T(8,128)}) custom-call(f32[384,384]{1,0:T(8,128)} %get-tuple-element.12.g00_ref, f32[384,384]{1,0:T(8,128)} %get-tuple-element.13.g10_ref, f32[384,384]{1,0:T(8,128)} %get-tuple-element.14.g11_ref), custom_call_target="tpu_custom_call" | custom-call | flops 452984832 | bytes 4718592 | tf_op jit(solution)/shard_map/pallas_call | solution.py:87
  435.0 5.4 %fusion.23 = f32[1536,384]{0,1:T(8,128)} fusion(f32[1536,384]{1,0:T(8,128)} %get-tuple-element.18, f32[384,384]{1,0:T(8,128)} %get-tuple-element.7), kind=kOutput, calls=%fused_computation.39 | convolution fusion | flops 1358954496 | bytes 5308416 | tf_op jit(solution)/shard_map/dot_general | solution.py:125
  440.4 0.0 copy-done.9
  440.4 3.6 fusion.15
  443.9 3.5 copy.12
  447.5 5.8 %convolution_subtract_fusion = f32[1536,384]{1,0:T(8,128)S(1)} fusion(f32[1536,384]{1,0:T(8,128)S(1)} %copy-done, f32[1536,384]{0,1:T(8,128)} %fusion.23, f32[384,384]{1,0:T(8,128)S(1)} %copy-done.13), kind=kOutput, calls=%fused_computation.10 | convolution fusion | flops 1359544320 | bytes 7667712 | tf_op jit(solution)/shard_map/dot_general | solution.py:126
  453.3 3.5 fusion.24
  456.8 3.2 copy.11
  460.1 2.1 fusion.12
  462.2 2.1 fusion.10
  464.4 3.6 select_bitcast_fusion.1
  467.9 2.1 select_bitcast_fusion
  470.1 0.0 copy-start.2
  470.1 0.0 slice-start.3
  470.1 3.4 pad_maximum_fusion
  473.5 0.0 slice-start.5
  473.5 15.0 %fusion.2 = f32[1536,4,384]{2,0,1:T(8,128)S(1)} fusion(f32[1536,384]{0,1:T(8,128)S(1)} %copy-done.6, f32[1536,384]{0,1:T(8,128)S(1)} %copy-done.2, f32[768,4,384]{2,1,0:T(4,128)} %pad_maximum_fusion), kind=kOutput, calls=%fused_computation.4 | convolution fusion | flops 10872815616 | bytes 18874368 | tf_op jit(solution)/shard_map/mb,bjt->mjt/dot_general | solution.py:132
  488.6 3.3 pad_maximum_fusion.1
  491.9 24.5 %fusion.1 = f32[1536,4,384]{2,1,0:T(4,128)} fusion(f32[1536,4,384]{2,1,0:T(4,128)S(1)} %bitcast.43, f32[1536,4,384]{2,0,1:T(8,128)S(1)} %fusion.2, f32[1536,384]{1,0:T(8,128)S(1)} %copy-done.4, f32[1536,384]{1,0:T(8,128)S(1)} %copy-done.5, pred[4]{0:T(512)(128)(4,1)S(1)} %get-tuple-element.27, pred[4]{0:T(512)(128)(4,1)S(1)} %get-tuple-element.28), kind=kLoop, calls=%fused_computation.2 | loop fusion | flops 7077888 | bytes 33030152 | tf_op jit(solution)/shard_map/jit(_where)/select_n | solution.py:134
  (46 shorter events, 0.1 us)
Async XLA Ops:
  7.2 124.9 %all-reduce.7.cloned.1.call-start = ((), (), s32[]{:S(2)}) async-start(), calls=%async_computation.1 | async-start | bytes 9437184 | tf_op jit(solution)/shard_map/psum | solution.py:109
  14.0 137.8 %slice-start = ((s8[9437184]{0:T(1024)(128)(4,1)}), s8[1048576]{0:T(1024)(128)(4,1)S(1)}, s32[]{:S(2)}) async-start(s8[9437184]{0:T(1024)(128)(4,1)} %bitcast.40), calls=%async_computation.2 | async-start | bytes 2097152
  14.0 324.3 %all-reduce.5.cloned.1.call-start = ((), (), s32[]{:S(2)}) async-start(), calls=%async_computation | async-start | bytes 12976128 | tf_op jit(solution)/shard_map/psum | solution.py:120
  132.1 14.5 %copy-start.1 = (f32[1536,384]{1,0:T(8,128)S(1)}, f32[1536,384]{1,0:T(8,128)}, u32[]{:S(2)}) copy-start(f32[1536,384]{1,0:T(8,128)} %get-tuple-element.18) | copy-start | bytes 7077892
  132.1 19.7 %slice-start.1 = ((s8[9437184]{0:T(1024)(128)(4,1)}), s8[4194304]{0:T(1024)(128)(4,1)S(1)}, s32[]{:S(2)}) async-start(s8[9437184]{0:T(1024)(128)(4,1)} %bitcast.40), calls=%async_computation.3 | async-start | bytes 8388608
  139.4 12.5 %slice-start.2 = ((s8[9437184]{0:T(1024)(128)(4,1)}), s8[4194304]{0:T(1024)(128)(4,1)S(1)}, s32[]{:S(2)}) async-start(s8[9437184]{0:T(1024)(128)(4,1)} %bitcast.40), calls=%async_computation.4 | async-start | bytes 8388608
  146.6 5.2 copy-start
  435.0 5.4 %copy-start.9 = (f32[384,4,384]{2,0,1:T(8,128)S(1)}, f32[384,4,384]{2,0,1:T(8,128)}, u32[]{:S(2)}) copy-start(f32[384,4,384]{2,0,1:T(8,128)} %get-tuple-element.16) | copy-start | bytes 7077892
  435.0 5.4 %copy-start.10 = (f32[384,384]{1,0:T(8,128)S(1)}, f32[384,384]{1,0:T(8,128)}, u32[]{:S(2)}) copy-start(f32[384,384]{1,0:T(8,128)} %get-tuple-element.7) | copy-start | bytes 1769476
  443.9 3.5 copy-start.13
  447.4 5.8 %copy-start.11 = (f32[384,384]{1,0:T(8,128)S(1)}, f32[384,384]{1,0:T(8,128)}, u32[]{:S(2)}) copy-start(f32[384,384]{1,0:T(8,128)} %get-tuple-element.9) | copy-start | bytes 1769476
  456.8 3.2 copy-start.3
  456.8 3.2 copy-start.14
  460.1 2.1 copy-start.8
  460.1 2.1 copy-start.12
  462.2 2.1 copy-start.16
  464.3 3.6 copy-start.15
  470.1 3.4 copy-start.2
  470.1 3.4 copy-start.6
  470.1 21.8 %slice-start.3 = ((s8[9437184]{0:T(1024)(128)(4,1)}), s8[1048576]{0:T(1024)(128)(4,1)S(1)}, s32[]{:S(2)}) async-start(s8[9437184]{0:T(1024)(128)(4,1)} %bitcast.42), calls=%async_computation.5 | async-start | bytes 2097152
  473.5 15.1 %copy-start.7 = (f32[1,384,4,384]{3,2,1,0:T(4,128)S(1)}, f32[1,384,4,384]{3,2,1,0:T(4,128)}, u32[]{:S(2)}) copy-start(f32[1,384,4,384]{3,2,1,0:T(4,128)} %get-tuple-element.19) | copy-start | bytes 7077892
  473.5 18.4 %slice-start.4 = ((s8[9437184]{0:T(1024)(128)(4,1)}), s8[4194304]{0:T(1024)(128)(4,1)S(1)}, s32[]{:S(2)}) async-start(s8[9437184]{0:T(1024)(128)(4,1)} %bitcast.42), calls=%async_computation.6 | async-start | bytes 8388608
  473.5 18.4 %slice-start.5 = ((s8[9437184]{0:T(1024)(128)(4,1)}), s8[4194304]{0:T(1024)(128)(4,1)S(1)}, s32[]{:S(2)}) async-start(s8[9437184]{0:T(1024)(128)(4,1)} %bitcast.42), calls=%async_computation.7 | async-start | bytes 8388608
  488.6 3.3 copy-start.4
  488.6 3.3 copy-start.5
Sparse Core Ops, SparseCore 0:
  14.1 117.9 all-reduce.6
  168.5 169.7 all-reduce.4

commit v8 on v7

--- a/solution.py
+++ b/solution.py
@@ -104,7 +104,7 @@
     count = matrix.shape[1]
     width = matrix.shape[2]
     glob = jnp.arange(count, dtype=jnp.int32) * ncol + column
-    own = matrix[:, 0, :]
+    own = with_layout_constraint(matrix, Layout(major_to_minor=(0, 1, 2)))[:, 0, :]
     zero = jnp.zeros_like(own)
     panel0, panel1 = lax.psum(
         (jnp.where(column == 0, own, zero), jnp.where(column == 1, own, zero)), "col"

time: 533 us -> 534 us (level)
  no operation moved by 1% of the time
where the time goes in v8:
time: 534 us; the launch traced here: 524 us
  waiting for transfers between devices  288 us (54%)
  Pallas kernels  96.7 us (18%)
  matrix products  72.5 us (14%)
  other arithmetic  43.5 us (8%)
  between operations  14.5 us (3%)
  local copies, waits for them, and re-layouts  9.32 us (2%)
    psum x1, waiting for transfers between devices, shards(): g00, g10, g11, cross0, cross1 = lax.psum(parts, 'row')  170 us
    psum x1, waiting for transfers between devices, shards(): lax.psum((jnp.where(column == 0, own, zero), jnp.where(column == 1, own,...  118 us
    pallas_call x1, Pallas kernels, factor_pair(): pl.pallas_call(_pair_kernel, out_shape=(square,) * 5, scratch_shapes=[plt...  96.7 us
    select_n x1, other arithmetic, shards(): blocks = jnp.where((glob == 1)[None, :, None], basis1[:, None, :], blocks)  24.5 us
    dot_general x1, matrix products, shards(): blocks = matrix - jnp.einsum('mb,bjt->mjt', basis, kept, precision=high)  16.3 us
  transfers between devices with their start and end apart: 2, of which 2 were waited for; matrix products, arithmetic and copies ran while one was open for 0% of the time, Pallas kernels for 0%

profile of v8, /device:TPU:0, one launch (start us, length us, event | category | flops | bytes accessed | tf_op | source)
XLA Modules:
  0.0 524.4 jit_solution(6566165768838036536)
XLA Ops:
  7.2 0.0 all-reduce.7.cloned.1.call-start
  7.2 6.6 %broadcast_select_fusion = (f32[1536,1,384]{2,1,0:T(1,128)S(1)}, f32[1536,1,384]{2,1,0:T(1,128)S(1)}) fusion(pred[]{:T(512)S(6)} %eq.24, f32[1536,4,384]{2,1,0:T(4,128)} %param.1, pred[]{:T(512)S(6)} %eq.23), kind=kLoop, calls=%fused_computation.14 | loop fusion | flops 1179648 | bytes 7077890 | tf_op jit(solution)/shard_map/jit(_where)/select_n | solution.py:110
  13.8 2.5 copy_bitcast_fusion
  16.3 0.0 all-reduce.7.cloned.1.call-update
  16.3 0.0 all-reduce.5.cloned.1.call-start
  16.4 118.0 %all-reduce.7.cloned.1.call-done = (f32[1536,384]{1,0:T(8,128)}, f32[1536,384]{1,0:T(8,128)}) async-done(((f32[1536,384]{1,0:T(8,128)}, f32[1536,384]{1,0:T(8,128)}), (f32[1536,384]{1,0:T(8,128)}, f32[1536,384]{1,0:T(8,128)})) %all-reduce.7.cloned.1.call-update) | async-done | bytes 4718608 | tf_op jit(solution)/shard_map/psum | solution.py:109
  134.4 7.2 %fusion.22 = f32[384,384]{1,0:T(8,128)} fusion(f32[1536,384]{1,0:T(8,128)} %get-tuple-element.17), kind=kOutput, calls=%fused_computation.40 | convolution fusion | flops 2717908992 | bytes 2949120 | tf_op jit(solution)/shard_map/dot_general | solution.py:116
  141.7 4.8 fusion.21
  146.4 5.2 fusion.20
  151.6 8.1 %fusion.2 = f32[384,4,384]{2,0,1:T(8,128)} fusion(f32[1536,4,384]{2,1,0:T(4,128)S(1)} %copy-done.4, f32[1536,384]{1,0:T(8,128)S(1)} %copy-done), kind=kOutput, calls=%fused_computation.3 | convolution fusion | flops 5435817984 | bytes 14155776 | tf_op jit(solution)/shard_map/mb,mjt->bjt/dot_general | solution.py:118
  159.8 8.4 %fusion.4 = f32[384,4,384]{2,0,1:T(8,128)} fusion(f32[1536,4,384]{2,1,0:T(4,128)S(1)} %copy-done.4, f32[1536,384]{1,0:T(8,128)S(1)} %copy-done.1), kind=kOutput, calls=%fused_computation.5 | convolution fusion | flops 5435817984 | bytes 14155776 | tf_op jit(solution)/shard_map/mb,mjt->bjt/dot_general | solution.py:117
  168.2 0.0 all-reduce.5.cloned.1.call-update
  168.2 169.7 %all-reduce.5.cloned.1.call-done = (f32[384,384]{1,0:T(8,128)}, f32[384,384]{1,0:T(8,128)}, f32[384,384]{1,0:T(8,128)}, f32[384,4,384]{2,0,1:T(8,128)}, f32[384,4,384]{2,0,1:T(8,128)}) async-done(((f32[384,384]{1,0:T(8,128)}, f32[384,384]{1,0:T(8,128)}, f32[384,384]{1,0:T(8,128)}, f32[384,4,384]{2,0,1:T(8,128)}, f32[384,4,384]{2,0,1:T(8,128)}), (f32[384,384]{1,0:T(8,128)}, f32[384,384]{1,0:T(8,128)}, ...) | async-done | bytes 6488080 | tf_op jit(solution)/shard_map/psum | solution.py:120
  338.0 96.7 %shard_map.30 = (f32[384,384]{1,0:T(8,128)}, f32[384,384]{1,0:T(8,128)}, f32[384,384]{1,0:T(8,128)}, f32[384,384]{1,0:T(8,128)}, f32[384,384]{1,0:T(8,128)}) custom-call(f32[384,384]{1,0:T(8,128)} %get-tuple-element.12.g00_ref, f32[384,384]{1,0:T(8,128)} %get-tuple-element.13.g10_ref, f32[384,384]{1,0:T(8,128)} %get-tuple-element.14.g11_ref), custom_call_target="tpu_custom_call" | custom-call | flops 452984832 | bytes 4718592 | tf_op jit(solution)/shard_map/pallas_call | solution.py:87
  434.7 5.4 %fusion.23 = f32[1536,384]{0,1:T(8,128)} fusion(f32[1536,384]{1,0:T(8,128)} %get-tuple-element.18, f32[384,384]{1,0:T(8,128)} %get-tuple-element.7), kind=kOutput, calls=%fused_computation.41 | convolution fusion | flops 1358954496 | bytes 5308416 | tf_op jit(solution)/shard_map/dot_general | solution.py:125
  440.1 3.6 fusion.17
  443.6 3.5 copy.4
  447.2 5.8 %convolution_subtract_fusion = f32[1536,384]{1,0:T(8,128)S(1)} fusion(f32[1536,384]{1,0:T(8,128)S(1)} %copy-done, f32[1536,384]{0,1:T(8,128)} %fusion.23, f32[384,384]{1,0:T(8,128)S(1)} %copy-done.13), kind=kOutput, calls=%fused_computation.16 | convolution fusion | flops 1359544320 | bytes 7667712 | tf_op jit(solution)/shard_map/dot_general | solution.py:126
  453.0 3.5 fusion.24
  456.5 3.3 copy.3
  459.8 0.0 copy-done.3
  459.8 2.1 fusion.14
  461.9 2.1 fusion.12
  464.0 3.6 select_bitcast_fusion.1
  467.6 2.1 select_bitcast_fusion
  469.8 0.0 copy-start.2
  469.8 0.0 slice-start
  469.8 3.4 pad_maximum_fusion
  473.2 0.0 slice-start.2
  473.2 16.3 %fusion.6 = f32[1536,4,384]{2,0,1:T(8,128)S(1)} fusion(f32[1536,384]{0,1:T(8,128)S(1)} %copy-done.7, f32[1536,384]{0,1:T(8,128)S(1)} %copy-done.2, f32[768,4,384]{2,1,0:T(4,128)} %pad_maximum_fusion), kind=kOutput, calls=%fused_computation.8 | convolution fusion | flops 10872815616 | bytes 18874368 | tf_op jit(solution)/shard_map/mb,bjt->mjt/dot_general | solution.py:132
  489.6 3.3 pad_maximum_fusion.1
  492.9 24.5 %fusion.1 = f32[1536,4,384]{2,1,0:T(4,128)} fusion(f32[1536,4,384]{2,1,0:T(4,128)S(1)} %bitcast.41, f32[1536,4,384]{2,0,1:T(8,128)S(1)} %fusion.6, f32[1536,384]{1,0:T(8,128)S(1)} %copy-done.5, f32[1536,384]{1,0:T(8,128)S(1)} %copy-done.6, pred[4]{0:T(512)(128)(4,1)S(1)} %get-tuple-element.27, pred[4]{0:T(512)(128)(4,1)S(1)} %get-tuple-element.28), kind=kLoop, calls=%fused_computation.2 | loop fusion | flops 7077888 | bytes 33030152 | tf_op jit(solution)/shard_map/jit(_where)/select_n | solution.py:134
  (37 shorter events, 0.1 us)
Async XLA Ops:
  7.2 127.2 %all-reduce.7.cloned.1.call-start = ((), (), s32[]{:S(2)}) async-start(), calls=%async_computation.1 | async-start | bytes 9437184 | tf_op jit(solution)/shard_map/psum | solution.py:109
  16.3 321.7 %all-reduce.5.cloned.1.call-start = ((), (), s32[]{:S(2)}) async-start(), calls=%async_computation | async-start | bytes 12976128 | tf_op jit(solution)/shard_map/psum | solution.py:120
  134.4 7.2 %copy-start = (f32[1536,384]{1,0:T(8,128)S(1)}, f32[1536,384]{1,0:T(8,128)}, u32[]{:S(2)}) copy-start(f32[1536,384]{1,0:T(8,128)} %get-tuple-element.17) | copy-start | bytes 7077892
  134.4 7.2 %copy-start.1 = (f32[1536,384]{1,0:T(8,128)S(1)}, f32[1536,384]{1,0:T(8,128)}, u32[]{:S(2)}) copy-start(f32[1536,384]{1,0:T(8,128)} %get-tuple-element.18) | copy-start | bytes 7077892
  141.6 10.0 %copy-start.4 = (f32[1536,4,384]{2,1,0:T(4,128)S(1)}, f32[1536,4,384]{2,1,0:T(4,128)}, u32[]{:S(2)}) copy-start(f32[1536,4,384]{2,1,0:T(4,128)} %param.1) | copy-start | bytes 28311556
  434.7 5.4 %copy-start.10 = (f32[384,4,384]{2,0,1:T(8,128)S(1)}, f32[384,4,384]{2,0,1:T(8,128)}, u32[]{:S(2)}) copy-start(f32[384,4,384]{2,0,1:T(8,128)} %get-tuple-element.16) | copy-start | bytes 7077892
  434.7 5.4 %copy-start.11 = (f32[384,384]{1,0:T(8,128)S(1)}, f32[384,384]{1,0:T(8,128)}, u32[]{:S(2)}) copy-start(f32[384,384]{1,0:T(8,128)} %get-tuple-element.7) | copy-start | bytes 1769476
  443.6 3.5 copy-start.13
  447.2 5.8 %copy-start.12 = (f32[384,384]{1,0:T(8,128)S(1)}, f32[384,384]{1,0:T(8,128)}, u32[]{:S(2)}) copy-start(f32[384,384]{1,0:T(8,128)} %get-tuple-element.9) | copy-start | bytes 1769476
  456.5 3.3 copy-start.3
  459.8 2.1 copy-start.9
  461.9 2.1 copy-start.15
  464.0 3.6 copy-start.14
  469.8 3.5 copy-start.2
  469.8 3.4 copy-start.7
  469.8 23.1 %slice-start = ((s8[9437184]{0:T(1024)(128)(4,1)}), s8[4194304]{0:T(1024)(128)(4,1)S(1)}, s32[]{:S(2)}) async-start(s8[9437184]{0:T(1024)(128)(4,1)} %bitcast.40), calls=%async_computation.2 | async-start | bytes 8388608
  473.2 16.3 %copy-start.8 = (f32[1,384,4,384]{3,2,1,0:T(4,128)S(1)}, f32[1,384,4,384]{3,2,1,0:T(4,128)}, u32[]{:S(2)}) copy-start(f32[1,384,4,384]{3,2,1,0:T(4,128)} %get-tuple-element.19) | copy-start | bytes 7077892
  473.2 19.6 %slice-start.1 = ((s8[9437184]{0:T(1024)(128)(4,1)}), s8[4194304]{0:T(1024)(128)(4,1)S(1)}, s32[]{:S(2)}) async-start(s8[9437184]{0:T(1024)(128)(4,1)} %bitcast.40), calls=%async_computation.3 | async-start | bytes 8388608
  473.2 19.6 %slice-start.2 = ((s8[9437184]{0:T(1024)(128)(4,1)}), s8[1048576]{0:T(1024)(128)(4,1)S(1)}, s32[]{:S(2)}) async-start(s8[9437184]{0:T(1024)(128)(4,1)} %bitcast.40), calls=%async_computation.4 | async-start | bytes 2097152
  489.5 3.3 copy-start.5
  489.6 3.3 copy-start.6
Sparse Core Ops, SparseCore 0:
  16.4 117.9 all-reduce.6
  168.3 169.6 all-reduce.4

commit v9 on v7

--- a/solution.py
+++ b/solution.py
@@ -110,14 +110,17 @@
         (jnp.where(column == 0, own, zero), jnp.where(column == 1, own, zero)), "col"
     )
     high = lax.Precision.HIGH
+    both = jnp.concatenate([panel0, panel1], axis=1)
     parts = (
-        jnp.dot(panel0.T, panel0, precision=highest, preferred_element_type=jnp.float32),
-        jnp.dot(panel1.T, panel0, precision=highest, preferred_element_type=jnp.float32),
-        jnp.dot(panel1.T, panel1, precision=highest, preferred_element_type=jnp.float32),
-        jnp.einsum("mb,mjt->bjt", panel0, matrix, precision=high),
-        jnp.einsum("mb,mjt->bjt", panel1, matrix, precision=high),
+        jnp.dot(both.T, both, precision=highest, preferred_element_type=jnp.float32),
+        jnp.einsum("mb,mjt->bjt", both, matrix, precision=high),
     )
-    g00, g10, g11, cross0, cross1 = lax.psum(parts, "row")
+    gram, cross = lax.psum(parts, "row")
+    g00 = gram[:width, :width]
+    g10 = gram[width:, :width]
+    g11 = gram[width:, width:]
+    cross0 = cross[:width]
+    cross1 = cross[width:]
     upper0, inv0, xmat, upper1, inv1 = factor_pair(g00, g10, g11)
     proj0 = jnp.einsum("ab,bjt->ajt", inv0, cross0, precision=high)
     rest1 = cross1 - jnp.einsum("ab,bjt->ajt", xmat, proj0, precision=high)

time: 533 us -> 550 us (1.032)
  matrix products: 73.7 us -> 62.4 us
  Pallas kernels: 96.7 us -> 107 us
  other arithmetic: 39.4 us -> 46.7 us
  local copies, waits for them, and re-layouts: 11.1 us -> 17.6 us
    pallas_call x1, Pallas kernels: 96.7 us -> 107 us  [factor_pair(): pl.pallas_call(_pair_kernel, out_shape=(square,) * 5, scratch_shapes=[plt...]
    dot_general x5 -> x2, matrix products: 36.2 us -> 26.7 us  [the longest x1 13.5 us: shards(): jnp.einsum('mb,mjt->bjt', both, matrix, precision=high)]
    another operation x3, other arithmetic: 8.98 us -> 14.8 us  [shards(): jnp.stack([row0, row1])]
where the time goes in v9:
time: 550 us; the launch traced here: 541 us
  waiting for transfers between devices  293 us (53%)
  Pallas kernels  107 us (19%)
  matrix products  62.4 us (11%)
  other arithmetic  46.7 us (8%)
  local copies, waits for them, and re-layouts  17.6 us (3%)
  between operations  14.5 us (3%)
    psum x1, waiting for transfers between devices, shards(): gram, cross = lax.psum(parts, 'row')  175 us
    psum x1, waiting for transfers between devices, shards(): lax.psum((jnp.where(column == 0, own, zero), jnp.where(column == 1, own,...  118 us
    pallas_call x1, Pallas kernels, factor_pair(): pl.pallas_call(_pair_kernel, out_shape=(square,) * 5, scratch_shapes=[plt...  107 us
    select_n x1, other arithmetic, shards(): blocks = jnp.where((glob == 1)[None, :, None], basis1[:, None, :], blocks)  24.3 us
    dot_general x1, matrix products, shards(): blocks = matrix - jnp.einsum('mb,bjt->mjt', basis, kept, precision=high)  15.1 us
    another operation x3, other arithmetic, shards(): jnp.stack([row0, row1])  14.8 us
    dot_general x1, matrix products, shards(): jnp.einsum('mb,mjt->bjt', both, matrix, precision=high)  13.5 us
    dot_general x1, matrix products, shards(): jnp.dot(both.T, both, precision=highest, preferred_element_type=jnp.float32)  13.2 us
  transfers between devices with their start and end apart: 2, of which 2 were waited for; matrix products, arithmetic and copies ran while one was open for 0% of the time, Pallas kernels for 0%

profile of v9, /device:TPU:0, one launch (start us, length us, event | category | flops | bytes accessed | tf_op | source)
XLA Modules:
  0.0 541.2 jit_solution(1240620415213190585)
XLA Ops:
  7.2 0.0 all-reduce.7.cloned.1.call-start
  7.2 0.0 slice-start.6
  7.2 1.7 slice-done.6
  8.9 5.1 copy.14
  14.0 4.5 select_bitcast_fusion.2
  18.4 0.0 all-reduce.7.cloned.1.call-update
  18.5 0.0 all-reduce.5.cloned.1.call-start
  18.5 118.0 %all-reduce.7.cloned.1.call-done = (f32[1536,384]{0,1:T(8,128)}, f32[1536,384]{0,1:T(8,128)}) async-done(((f32[1536,384]{0,1:T(8,128)}, f32[1536,384]{0,1:T(8,128)}), (f32[1536,384]{0,1:T(8,128)}, f32[1536,384]{0,1:T(8,128)})) %all-reduce.7.cloned.1.call-update) | async-done | bytes 4718608 | tf_op jit(solution)/shard_map/psum | solution.py:109
  136.6 2.0 constant_dynamic-update-slice_fusion.1
  138.5 0.4 copy-done.3
  138.9 0.2 constant_dynamic-update-slice_fusion
  139.1 0.0 slice-start.1
  139.1 13.2 %fusion.18 = f32[768,768]{1,0:T(8,128)} fusion(f32[1536,768]{0,1:T(8,128)S(1)} %constant_dynamic-update-slice_fusion), kind=kOutput, calls=%fused_computation.37 | convolution fusion | flops 10871635968 | bytes 7077888 | tf_op jit(solution)/shard_map/dot_general | solution.py:115
  152.3 13.5 %fusion.2 = f32[768,4,384]{2,0,1:T(8,128)} fusion(f32[1536,4,384]{2,1,0:T(4,128)S(1)} %bitcast.33, f32[1536,768]{0,1:T(8,128)S(1)} %constant_dynamic-update-slice_fusion), kind=kOutput, calls=%fused_computation.3 | convolution fusion | flops 10871635968 | bytes 18874368 | tf_op jit(solution)/shard_map/mb,mjt->bjt/dot_general | solution.py:116
  165.8 0.0 all-reduce.5.cloned.1.call-update
  165.8 175.0 %all-reduce.5.cloned.1.call-done = (f32[768,768]{1,0:T(8,128)}, f32[768,4,384]{2,0,1:T(8,128)}) async-done(((f32[768,768]{1,0:T(8,128)}, f32[768,4,384]{2,0,1:T(8,128)}), (f32[768,768]{1,0:T(8,128)}, f32[768,4,384]{2,0,1:T(8,128)})) %all-reduce.5.cloned.1.call-update) | async-done | bytes 7077904 | tf_op jit(solution)/shard_map/psum | solution.py:118
  340.9 2.7 fusion.17
  343.6 106.8 %shard_map.30 = (f32[384,384]{1,0:T(8,128)}, f32[384,384]{1,0:T(8,128)}, f32[384,384]{1,0:T(8,128)}, f32[384,384]{1,0:T(8,128)}, f32[384,384]{1,0:T(8,128)}) custom-call(f32[384,384]{1,0:T(8,128)} %get-tuple-element.22.g00_ref, f32[384,384]{1,0:T(8,128)} %get-tuple-element.21.g10_ref, f32[384,384]{1,0:T(8,128)} %get-tuple-element.20.g11_ref), custom_call_target="tpu_custom_call" | custom-call | flops 452984832 | bytes 4718592 | tf_op jit(solution)/shard_map/pallas_call | solution.py:87
  450.4 3.8 fusion.19
  454.2 2.0 copy.5
  456.3 3.8 convolution_subtract_fusion
  460.1 3.9 fusion.10
  464.1 2.2 fusion.12
  466.3 3.5 fusion.20
  469.8 3.5 fusion.9
  473.2 3.5 copy.4
  476.8 5.4 select_bitcast_fusion.1
  482.2 3.6 select_bitcast_fusion
  485.8 3.2 pad_maximum_fusion
  489.0 15.1 %fusion.4 = f32[1536,4,384]{2,0,1:T(8,128)S(1)} fusion(f32[1536,384]{0,1:T(8,128)S(1)} %copy-done.4, f32[1536,384]{0,1:T(8,128)S(1)} %fusion.19, f32[768,4,384]{2,1,0:T(4,128)} %pad_maximum_fusion), kind=kOutput, calls=%fused_computation.6 | convolution fusion | flops 10872815616 | bytes 18874368 | tf_op jit(solution)/shard_map/mb,bjt->mjt/dot_general | solution.py:135
  504.1 5.8 %pad_maximum_fusion.1 = f32[2,384,4,384]{3,2,1,0:T(4,128)} fusion(f32[1,384,4,384]{3,2,1,0:T(4,128)} %get-tuple-element.18, f32[1,384,4,384]{3,2,1,0:T(4,128)} %get-tuple-element.16), kind=kLoop, calls=%fused_computation.10 | loop fusion | flops 1179648 | bytes 9437184 | tf_op jit(solution)/shard_map/stack | solution.py:141
  509.9 24.3 %fusion.1 = f32[1536,4,384]{2,1,0:T(4,128)} fusion(f32[1536,4,384]{2,1,0:T(4,128)S(1)} %bitcast.35, f32[1536,4,384]{2,0,1:T(8,128)S(1)} %fusion.4, f32[1536,384]{1,0:T(8,128)S(1)} %copy-done.1, f32[1536,384]{1,0:T(8,128)S(1)} %copy-done.2, pred[4]{0:T(512)(128)(4,1)S(1)} %get-tuple-element.27, pred[4]{0:T(512)(128)(4,1)S(1)} %get-tuple-element.28), kind=kLoop, calls=%fused_computation.2 | loop fusion | flops 7077888 | bytes 33030152 | tf_op jit(solution)/shard_map/jit(_where)/select_n | solution.py:137
  (41 shorter events, 0.1 us)
Async XLA Ops:
  7.2 129.4 %all-reduce.7.cloned.1.call-start = ((), (), s32[]{:S(2)}) async-start(), calls=%async_computation.1 | async-start | bytes 9437184 | tf_op jit(solution)/shard_map/psum | solution.py:109
  7.2 1.7 slice-start.6
  18.5 322.4 %all-reduce.5.cloned.1.call-start = ((), (), s32[]{:S(2)}) async-start(), calls=%async_computation | async-start | bytes 14155776 | tf_op jit(solution)/shard_map/psum | solution.py:118
  136.6 2.4 copy-start.3
  138.9 13.3 %slice-start = ((s8[9437184]{0:T(1024)(128)(4,1)}), s8[4194304]{0:T(1024)(128)(4,1)S(1)}, s32[]{:S(2)}) async-start(s8[9437184]{0:T(1024)(128)(4,1)} %bitcast.32), calls=%async_computation.2 | async-start | bytes 8388608
  139.1 13.2 %slice-start.1 = ((s8[9437184]{0:T(1024)(128)(4,1)}), s8[4194304]{0:T(1024)(128)(4,1)S(1)}, s32[]{:S(2)}) async-start(s8[9437184]{0:T(1024)(128)(4,1)} %bitcast.32), calls=%async_computation.3 | async-start | bytes 8388608
  139.1 13.2 %slice-start.2 = ((s8[9437184]{0:T(1024)(128)(4,1)}), s8[1048576]{0:T(1024)(128)(4,1)S(1)}, s32[]{:S(2)}) async-start(s8[9437184]{0:T(1024)(128)(4,1)} %bitcast.32), calls=%async_computation.4 | async-start | bytes 2097152
  454.2 2.0 copy-start.8
  456.2 3.8 copy-start.6
  460.1 9.7 %slice-start.7 = ((s8[4718592]{0:T(1024)(128)(4,1)}), s8[4194304]{0:T(1024)(128)(4,1)S(1)}, s32[]{:S(2)}) async-start(s8[4718592]{0:T(1024)(128)(4,1)} %bitcast.36), calls=%async_computation.9 | async-start | bytes 8388608
  464.0 2.2 copy-start
  464.0 2.2 copy-start.7
  464.0 5.7 %slice-start.8 = ((s8[4718592]{0:T(1024)(128)(4,1)}), s8[524288]{0:T(1024)(128)(4,1)S(1)}, s32[]{:S(2)}) async-start(s8[4718592]{0:T(1024)(128)(4,1)} %bitcast.36), calls=%async_computation.10 | async-start | bytes 1048576
  473.2 3.5 copy-start.10
  476.8 5.4 copy-start.5
  476.8 5.4 copy-start.9
  485.8 3.2 copy-start.4
  485.8 24.1 %slice-start.3 = ((s8[9437184]{0:T(1024)(128)(4,1)}), s8[1048576]{0:T(1024)(128)(4,1)S(1)}, s32[]{:S(2)}) async-start(s8[9437184]{0:T(1024)(128)(4,1)} %bitcast.34), calls=%async_computation.5 | async-start | bytes 2097152
  489.0 20.9 %slice-start.4 = ((s8[9437184]{0:T(1024)(128)(4,1)}), s8[4194304]{0:T(1024)(128)(4,1)S(1)}, s32[]{:S(2)}) async-start(s8[9437184]{0:T(1024)(128)(4,1)} %bitcast.34), calls=%async_computation.6 | async-start | bytes 8388608
  489.0 20.9 %slice-start.5 = ((s8[9437184]{0:T(1024)(128)(4,1)}), s8[4194304]{0:T(1024)(128)(4,1)S(1)}, s32[]{:S(2)}) async-start(s8[9437184]{0:T(1024)(128)(4,1)} %bitcast.34), calls=%async_computation.7 | async-start | bytes 8388608
  504.1 5.8 %copy-start.1 = (f32[1536,384]{1,0:T(8,128)S(1)}, f32[1536,384]{1,0:T(8,128)}, u32[]{:S(2)}) copy-start(f32[1536,384]{1,0:T(8,128)} %copy.5) | copy-start | bytes 7077892
  504.1 5.8 %copy-start.2 = (f32[1536,384]{1,0:T(8,128)S(1)}, f32[1536,384]{1,0:T(8,128)}, u32[]{:S(2)}) copy-start(f32[1536,384]{1,0:T(8,128)} %copy.4) | copy-start | bytes 7077892
Sparse Core Ops, SparseCore 0:
  18.6 117.9 all-reduce.6
  165.9 174.8 all-reduce.4
